TPU v7x, 256 devices: a whole 4x4x8 slice. The times are simulated.
256 devices in a mesh: gx: 16 (over z, core), gy: 4 (over x), gz: 4 (over y).
Axes of the slice: x: 4, y: 4, z: 8, core: 2. Of those that a mesh axis runs over, the one named last changes fastest.
Arguments:
- fields: float32 [5, 512, 256, 512], P(None, 'gx', 'gy', 'gz'), may hold values from -4 to 9
- viscous: float32 [5], replicated, may hold values from 1 to 8000
Outputs:
- updated: float32 [5, 512, 256, 512], P(None, 'gx', 'gy', 'gz')
All inputs are finite; a program needn't handle non-finite values.
Results may differ from a plain program's by a relative error of at most 0.0003.
Values sent between devices are 32-bit elements; how exact they have to be, the bound alone decides.
No kernel may reach another device: no remote copies, remote signals or barrier semaphores. Data moves between devices by JAX's collectives and lax.ppermute only.
A program may use at most 128 MiB of HBM per device.

v0:
```python
import math

import jax
import jax.numpy as jnp
from jax import lax
from jax.experimental import pallas as pl
from jax.sharding import PartitionSpec as P

advect = 0.3
root_ratio = (-1.0 + math.sqrt(5.0) / 3.0) * 1.5
line_gain = (1.0 + root_ratio * root_ratio) / (1.0 - root_ratio * root_ratio)
highest = lax.Precision.HIGHEST


def signed_power(exponent):
    parity = jnp.mod(exponent, 2.0)
    return (1.0 - 2.0 * parity) * jnp.exp(exponent * math.log(abs(root_ratio)))


def span_weights(offset):
    weights = {1: 45.0, -1: -45.0, 2: -9.0, -2: 9.0, 3: 1.0, -3: -1.0}
    return sum((w / 60.0) * (offset == k).astype(jnp.float32) for k, w in weights.items())


def span_halos(fields):
    cols = fields.shape[3]
    lanes = jnp.arange(cols)
    halo = jnp.arange(3)
    pick = jnp.concatenate(
        [lanes[None, :] == cols - 3 + halo[:, None], lanes[None, :] == halo[:, None]]
    ).astype(jnp.float32)
    edges = jnp.einsum("cz,fxyz->fxcy", pick, fields, precision=highest)
    return shifted_in(edges[:, :, :3], "gz", 1), shifted_in(edges[:, :, 3:], "gz", -1)


def span_inner(fields):
    lanes = jnp.arange(fields.shape[3])
    interior = span_weights(lanes[:, None] - lanes[None, :])
    return jnp.einsum("fxyw,wz->fxyz", fields, interior, precision=highest)


def span_halo_term(before, after, cols):
    lanes = jnp.arange(cols)
    halo = jnp.arange(3)
    weights = jnp.concatenate(
        [span_weights(halo[:, None] - 3 - lanes[None, :]), span_weights(halo[:, None] + cols - lanes[None, :])]
    )
    stacked = jnp.concatenate([before, after], axis=2)
    return jnp.einsum("fxcy,cz->fxyz", stacked, weights, precision=highest)

def wall_pivots(viscous, total_rows):
    root = jnp.sqrt(1.0 + 4.0 * viscous)
    upper = 0.5 * (1.0 + 2.0 * viscous + root)
    log_ratio = -2.0 * jnp.log1p((1.0 + root) / (2.0 * viscous))
    rows = jnp.arange(total_rows, dtype=jnp.float32)[None, :]
    ratio_rise = jnp.expm1((rows + 1.0) * log_ratio[:, None])
    ratio_next = jnp.expm1((rows + 2.0) * log_ratio[:, None])
    return ratio_rise / (ratio_next * upper[:, None])


def carried_over(line, gains, place, count, reverse):
    step = -1 if reverse else 1
    total = jnp.zeros_like(line)
    factor = jnp.ones_like(gains[0])
    for hop in range(1, count):
        pairs = [(i, i + step * hop) for i in range(count) if 0 <= i + step * hop < count]
        arrived = lax.ppermute(line, "gy", pairs)
        total = total + factor[:, None, None] * arrived
        between = jnp.clip(place - step * hop, 0, count - 1)
        factor = factor * lax.dynamic_index_in_dim(gains, between, 0, False)
    return total


def wall_carries(explicit, viscous):
    row_count = explicit.shape[2]
    count = lax.axis_size("gy")
    place = lax.axis_index("gy")
    total_rows = row_count * count
    all_pivots = wall_pivots(viscous, total_rows)
    all_log_gain = jnp.log(viscous[:, None] * all_pivots).reshape(viscous.shape[0], count, row_count)
    gains = jnp.exp(jnp.sum(all_log_gain, axis=2)).T
    pivots = lax.dynamic_index_in_dim(all_pivots.reshape(-1, count, row_count), place, 1, False)
    log_gain = lax.dynamic_index_in_dim(all_log_gain, place, 1, False)
    inclusive = jnp.cumsum(log_gain, axis=1)
    exclusive = inclusive - log_gain
    row_index = jnp.arange(row_count)[:, None]
    col_index = jnp.arange(row_count)[None, :]
    lower_mask = col_index <= row_index
    upper_mask = col_index >= row_index
    spread = inclusive[:, :, None] - inclusive[:, None, :]
    forward_table = jnp.where(
        lower_mask, pivots[:, None, :] * jnp.exp(jnp.where(lower_mask, spread, 0.0)), 0.0
    )
    eliminated_local = jnp.einsum("fik,fxkz->fxiz", forward_table, explicit, precision=highest)
    enter_low = carried_over(eliminated_local[:, :, -1], gains, place, count, False)
    eliminated = eliminated_local + jnp.exp(inclusive)[:, None, :, None] * enter_low[:, :, None, :]
    reach_log = exclusive[:, None, :] - exclusive[:, :, None]
    backward_table = jnp.where(upper_mask, jnp.exp(jnp.where(upper_mask, reach_log, 0.0)), 0.0)
    solved = jnp.einsum("fik,fxkz->fxiz", backward_table, eliminated, precision=highest)
    enter_high = carried_over(solved[:, :, 0], gains, place, count, True)
    trailing = jnp.exp(inclusive[:, -1:] - exclusive)
    return solved + trailing[:, None, :, None] * enter_high[:, :, None, :]


def shifted_in(array, axis, shift):
    peers = lax.axis_size(axis)
    return lax.ppermute(array, axis, [(i, (i + shift) % peers) for i in range(peers)])


def line_kernel(fields_ref, before_ref, after_ref, local_ref, moments_ref):
    length = fields_ref.shape[1]

    def plane(k):
        if k < 0:
            return before_ref[0, k + 2]
        if k >= length:
            return after_ref[0, k - length]
        return fields_ref[0, k]

    def source(i):
        return 7.0 / 9.0 * (plane(i + 1) - plane(i - 1)) + 1.0 / 36.0 * (plane(i + 2) - plane(i - 2))

    running = jnp.zeros(fields_ref.shape[2:], jnp.float32)
    for i in range(length):
        running = source(i) + root_ratio * running
        local_ref[0, i] = running
    moments_ref[0, 0] = running
    running = jnp.zeros(fields_ref.shape[2:], jnp.float32)
    for i in reversed(range(length)):
        value = source(i)
        running = value + root_ratio * running
        local_ref[0, i] = line_gain * (local_ref[0, i] + running - value)
    moments_ref[0, 1] = running


def line_local(fields, before, after):
    count, length, rows, cols = fields.shape
    block = lambda depth: pl.BlockSpec((1, depth, rows, cols), lambda f: (f, 0, 0, 0))
    size = fields.size * 4
    return pl.pallas_call(
        line_kernel,
        grid=(count,),
        in_specs=[block(length), block(2), block(2)],
        out_specs=[block(length), block(2)],
        out_shape=[
            jax.ShapeDtypeStruct(fields.shape, jnp.float32),
            jax.ShapeDtypeStruct((count, 2, rows, cols), jnp.float32),
        ],
        cost_estimate=pl.CostEstimate(flops=20 * fields.size, bytes_accessed=2 * size, transcendentals=0),
    )(fields, before, after)


def shards(fields, viscous):
    length = fields.shape[1]
    peers = lax.axis_size("gx")
    total = length * peers
    before = shifted_in(fields[:, length - 2 :], "gx", 1)
    after = shifted_in(fields[:, :2], "gx", -1)
    local, moments = line_local(fields, before, after)
    late, local, moments = lax.optimization_barrier((fields, local, moments))
    block_weight = root_ratio**length
    arrived = (
        shifted_in(moments[:, 0], "gx", 1),
        shifted_in(moments[:, 0], "gx", 2),
        shifted_in(moments[:, 1], "gx", -1),
        shifted_in(moments[:, 1], "gx", -2),
    )
    state = {"halos": span_halos(late)}
    state, arrived = lax.optimization_barrier((state, arrived))
    left = arrived[0] + block_weight * arrived[1]
    right = arrived[2] + block_weight * arrived[3]
    spans = []
    span = 2
    while span < peers:
        spans.append(span)
        span *= 2

    def inner_part(state):
        inner = span_inner(late)
        state["partial"] = late - advect * late[0] * local - advect * late[2] * inner

    def halo_part(state):
        halo_term = span_halo_term(*state["halos"], late.shape[3])
        state["partial"] = state["partial"] - advect * late[2] * halo_term

    tasks = [inner_part, halo_part]
    for span in spans:
        state, left, right = lax.optimization_barrier((state, left, right))
        from_left = shifted_in(left, "gx", span)
        from_right = shifted_in(right, "gx", -span)
        if tasks and span != spans[-1]:
            tasks.pop(0)(state)
        elif span == spans[-1]:
            while tasks:
                tasks.pop(0)(state)
        state, from_left, from_right = lax.optimization_barrier((state, from_left, from_right))
        weight = root_ratio ** (length * span)
        left = left + weight * from_left
        right = right + weight * from_right
    while tasks:
        tasks.pop(0)(state)
    index = jnp.arange(length, dtype=jnp.float32)
    wrap = line_gain * root_ratio / (1.0 - root_ratio**total)
    rising = signed_power(index)[None, :, None, None]
    falling = signed_power(length - 1 - index)[None, :, None, None]
    carried = wrap * (rising * left[:, None] + falling * right[:, None])
    explicit = state["partial"] - advect * fields[0] * carried
    updated = wall_carries(explicit, viscous)
    return updated


def solution(mesh):
    in_specs = (P(None, "gx", "gy", "gz"), P())
    out_specs = P(None, "gx", "gy", "gz")
    return jax.shard_map(shards, mesh=mesh, in_specs=in_specs, out_specs=out_specs, check_vma=False)
```

profile of v0, /device:TPU:24, one launch (start us, length us, event | category | flops | bytes accessed | tf_op | source)
XLA Modules:
  0.0 141.8 jit_solution(6890635531790376232)
XLA Ops:
  0.0 1.1 fusion.135
  1.1 0.0 collective-permute-start
  1.1 5.3 %collective-permute-start.1 = (f32[5,2,64,128]{3,2,1,0:T(8,128)S(1)}, f32[5,2,64,128]{3,2,1,0:T(8,128)S(1)}, u32[]{:S(2)}, u32[]{:S(2)}) collective-permute-start(f32[5,2,64,128]{3,2,1,0:T(8,128)S(1)} %get-tuple-element.81), channel_id=1, source_target_pairs={{0,240},{16,0},{32,16},{48,32},{64,48},{80,64},{96,80},{112,96},{1... | collective-permute-start | bytes 983048 | tf_op jit(solution)/shard_map/ppermute | solution.py:107
  6.5 0.7 log-plus-one_multiply_fusion
  7.2 0.8 fusion.132
  8.0 0.2 reduce_window_sum.13
  8.2 0.2 slice_reduce_fusion
  8.4 0.1 iota_compare_fusion.2
  8.5 0.1 subtract_exponential_fusion
  8.6 0.1 select_add_fusion
  8.7 1.3 multiply_bitcast_fusion
  10.0 1.2 collective-permute-done.before_ref
  11.2 0.0 collective-permute-done.1.after_ref
  11.2 0.7 copy-done
  11.9 0.7 copy-done.1
  12.6 8.1 %shard_map.28 = (f32[5,32,64,128]{3,2,1,0:T(8,128)}, f32[5,2,64,128]{3,2,1,0:T(8,128)}) custom-call(f32[5,32,64,128]{3,2,1,0:T(8,128)} %fields_ref.1, f32[5,2,64,128]{3,2,1,0:T(8,128)} %copy-done, f32[5,2,64,128]{3,2,1,0:T(8,128)} %copy-done.1), custom_call_target="tpu_custom_call" | custom-call | flops 26214400 | bytes 10485760 | tf_op jit(solution)/shard_map/pallas_call | solution.py:140
  20.7 0.9 slice_bitcast_fusion
  21.7 0.0 collective-permute-start.4
  21.7 0.1 collective-permute-start.5
  21.8 0.9 slice_bitcast_fusion.1
  22.7 2.9 %collective-permute-start.6 = (f32[5,64,128]{2,1,0:T(8,128)S(1)}, f32[5,64,128]{2,1,0:T(8,128)S(1)}, u32[]{:S(2)}, u32[]{:S(2)}) collective-permute-start(f32[5,64,128]{2,1,0:T(8,128)S(1)} %slice_bitcast_fusion.1), channel_id=1, source_target_pairs={{0,240},{16,0},{32,16},{48,32},{64,48},{80,64},{96,80},{112,96},{1... | collective-permute-start | bytes 491528 | tf_op jit(solution)/shard_map/ppermute | solution.py:107
  25.6 1.7 %collective-permute-start.7 = (f32[5,64,128]{2,1,0:T(8,128)S(1)}, f32[5,64,128]{2,1,0:T(8,128)S(1)}, u32[]{:S(2)}, u32[]{:S(2)}) collective-permute-start(f32[5,64,128]{2,1,0:T(8,128)S(1)} %slice_bitcast_fusion.1), channel_id=1, source_target_pairs={{0,224},{16,240},{32,0},{48,16},{64,32},{80,48},{96,64},{112,80},{... | collective-permute-start | bytes 491528 | tf_op jit(solution)/shard_map/ppermute | solution.py:107
  27.3 8.7 %convolution_bitcast_fusion = f32[5,32,6,64]{3,2,1,0:T(8,128)S(1)} fusion(f32[5,32,64,128]{3,2,1,0:T(8,128)} %fields_ref.1, pred[3,128]{1,0:T(4,128)(4,1)S(1)} %get-tuple-element.95, pred[3,128]{1,0:T(4,128)(4,1)S(1)} %get-tuple-element.96), kind=kOutput, calls=%fused_computation.21 | convolution fusion | flops 94372608 | bytes 5489408 | tf_op jit(solution)/shard_map/cz,fxyz->fxcy/dot_general | solution.py:32
  36.0 0.1 fusion.136
  36.1 0.0 slice-start
  36.2 0.0 slice-start.1
  36.2 0.3 collective-permute-start.2
  36.5 7.9 %fusion.45 = f32[5,32,64,128]{3,2,1,0:T(8,128)} fusion(f32[5,32,64,128]{3,2,1,0:T(8,128)} %fields_ref.1), kind=kOutput, calls=%fused_computation.60 | convolution fusion | flops 2013560832 | bytes 10485760 | tf_op jit(solution)/shard_map/fxyw,wz->fxyz/dot_general | solution.py:39
  44.4 0.4 collective-permute-done.2
  44.7 1.5 %collective-permute-start.3 = (f32[5,32,3,64]{3,2,1,0:T(4,128)S(1)}, f32[5,32,3,64]{3,2,1,0:T(4,128)S(1)}, u32[]{:S(2)}, u32[]{:S(2)}) collective-permute-start(f32[5,32,3,64]{3,2,1,0:T(4,128)S(1)} %get-tuple-element.83), channel_id=1, source_target_pairs={{0,3},{1,0},{2,1},{3,2},{4,7},{5,4},{6,5},{7,6},{8,11},{9,8},{10,9... | collective-permute-start | bytes 368648 | tf_op jit(solution)/shard_map/ppermute | solution.py:107
  46.2 1.3 multiply_bitcast_fusion.2
  47.5 6.4 %collective-permute-done.3 = f32[5,32,3,64]{3,2,1,0:T(4,128)S(1)} collective-permute-done((f32[5,32,3,64]{3,2,1,0:T(4,128)S(1)}, f32[5,32,3,64]{3,2,1,0:T(4,128)S(1)}, u32[]{:S(2)}, u32[]{:S(2)}) %collective-permute-start.3) | collective-permute-done | bytes 122912 | tf_op jit(solution)/shard_map/ppermute | solution.py:107
  53.8 0.0 collective-permute-done.5
  53.8 0.0 collective-permute-done.6
  53.9 0.7 copy-done.2
  54.6 0.0 collective-permute-done.7
  54.6 0.1 collective-permute-start.8
  54.7 3.2 %collective-permute-start.9 = (f32[5,64,128]{2,1,0:T(8,128)S(1)}, f32[5,64,128]{2,1,0:T(8,128)}, u32[]{:S(2)}, u32[]{:S(2)}) collective-permute-start(f32[5,64,128]{2,1,0:T(8,128)S(1)} %multiply_add_fusion.7), channel_id=1, source_target_pairs={{0,224},{16,240},{32,0},{48,16},{64,32},{80,48},{96,64},{112,80},{... | collective-permute-start | bytes 491528 | tf_op jit(solution)/shard_map/ppermute | solution.py:107
  57.9 8.8 %multiply_subtract_fusion.1 = f32[5,32,64,128]{3,2,1,0:T(8,128)} fusion(f32[5,32,64,128]{3,2,1,0:T(8,128)} %fusion.45, f32[5,32,64,128]{3,2,1,0:T(8,128)S(1)} %bitcast.72, f32[5,32,64,128]{3,2,1,0:T(8,128)} %get-tuple-element.51, f32[32,64,128]{2,1,0:T(8,128)S(1)} %get-tuple-element.80, f32[32,64,128]{2,1,0:T(8,128)} %get-tuple-element.79), kind=kLoop, calls=%fused_computation.11 | loop fusion | flops 5242880 | bytes 23068672 | tf_op jit(solution)/shard_map/sub | solution.py:180
  66.8 0.9 multiply_add_fusion.5
  67.7 2.5 %collective-permute-start.10 = (f32[5,64,128]{2,1,0:T(8,128)S(1)}, f32[5,64,128]{2,1,0:T(8,128)S(1)}, u32[]{:S(2)}, u32[]{:S(2)}) collective-permute-start(f32[5,64,128]{2,1,0:T(8,128)S(1)} %multiply_add_fusion.6), channel_id=1, source_target_pairs={{0,64},{16,80},{32,96},{48,112},{64,128},{80,144},{96,160},{112,17... | collective-permute-start | bytes 491528 | tf_op jit(solution)/shard_map/ppermute | solution.py:107
  70.3 1.7 %collective-permute-start.11 = (f32[5,64,128]{2,1,0:T(8,128)S(1)}, f32[5,64,128]{2,1,0:T(8,128)S(1)}, u32[]{:S(2)}, u32[]{:S(2)}) collective-permute-start(f32[5,64,128]{2,1,0:T(8,128)S(1)} %multiply_add_fusion.5), channel_id=1, source_target_pairs={{0,192},{16,208},{32,224},{48,240},{64,0},{80,16},{96,32},{112,48}... | collective-permute-start | bytes 491528 | tf_op jit(solution)/shard_map/ppermute | solution.py:107
  71.9 12.0 %multiply_subtract_fusion = f32[5,32,64,128]{3,2,1,0:T(8,128)} fusion(f32[5,32,64,128]{3,2,1,0:T(8,128)} %multiply_subtract_fusion.1, f32[32,64,128]{2,1,0:T(8,128)S(1)} %get-tuple-element.80, f32[5,32,3,64]{3,2,1,0:T(4,128)} %copy-done.2, f32[5,32,3,64]{3,2,1,0:T(4,128)S(1)} %collective-permute-done.2, f32[3,128]{1,0:T(4,128)S(1)} %get-tuple-element.97, ...), kind=kOutput, calls=%fused_computation.10 | convolution fusion | flops 97055488 | bytes 11783168 | tf_op jit(solution)/shard_map/fxcy,cz->fxyz/dot_general | solution.py:49
  84.1 4.9 %collective-permute-start.12 = (f32[5,64,128]{2,1,0:T(8,128)S(1)}, f32[5,64,128]{2,1,0:T(8,128)S(1)}, u32[]{:S(2)}, u32[]{:S(2)}) collective-permute-start(f32[5,64,128]{2,1,0:T(8,128)S(1)} %multiply_add_fusion.4), channel_id=1, source_target_pairs={{0,128},{16,144},{32,160},{48,176},{64,192},{80,208},{96,224},{112... | collective-permute-start | bytes 491528 | tf_op jit(solution)/shard_map/ppermute | solution.py:107
  89.0 1.1 collective-permute-start.13
  90.1 7.6 %collective-permute-done.12 = f32[5,64,128]{2,1,0:T(8,128)S(1)} collective-permute-done((f32[5,64,128]{2,1,0:T(8,128)S(1)}, f32[5,64,128]{2,1,0:T(8,128)S(1)}, u32[]{:S(2)}, u32[]{:S(2)}) %collective-permute-start.12) | collective-permute-done | bytes 163872 | tf_op jit(solution)/shard_map/ppermute | solution.py:107
  97.8 4.4 %collective-permute-done.13 = f32[5,64,128]{2,1,0:T(8,128)S(1)} collective-permute-done((f32[5,64,128]{2,1,0:T(8,128)S(1)}, f32[5,64,128]{2,1,0:T(8,128)S(1)}, u32[]{:S(2)}, u32[]{:S(2)}) %collective-permute-start.13) | collective-permute-done | bytes 163872 | tf_op jit(solution)/shard_map/ppermute | solution.py:107
  102.3 8.1 %fusion.16 = f32[5,32,64,128]{3,2,1,0:T(8,128)S(1)} fusion(f32[5,32,64,128]{3,2,1,0:T(8,128)} %multiply_subtract_fusion, f32[32,64,128]{2,1,0:T(8,128)S(1)} %multiply_bitcast_fusion, f32[5,64,128]{2,1,0:T(8,128)S(1)} %multiply_add_fusion.1, f32[32]{0:T(128)S(1)} %get-tuple-element.100, f32[5,64,128]{2,1,0:T(8,128)S(1)} %multiply_add_fusion.2, ...), kind=kOutput, calls=%fused_computation.19 | convolution fusion | flops 1013268480 | bytes 11868928 | tf_op jit(solution)/shard_map/fik,fxkz->fxiz/dot_general | solution.py:94
  110.4 0.1 slice.54
  110.5 4.7 %collective-permute-start.16 = (f32[5,32,128]{2,1,0:T(8,128)S(1)}, f32[5,32,128]{2,1,0:T(8,128)S(1)}, u32[]{:S(2)}, u32[]{:S(2)}) collective-permute-start(f32[5,32,128]{2,1,0:T(8,128)S(1)} %bitcast.73), channel_id=1, source_target_pairs={{0,12},{1,13},{2,14},{3,15},{16,28},{17,29},{18,30},{19,31},{32,44... | collective-permute-start | bytes 245768 | tf_op jit(solution)/shard_map/ppermute | solution.py:67
  115.2 1.3 collective-permute-start.14
  116.5 3.4 %collective-permute-start.15 = (f32[5,32,128]{2,1,0:T(8,128)S(1)}, f32[5,32,128]{2,1,0:T(8,128)S(1)}, u32[]{:S(2)}, u32[]{:S(2)}) collective-permute-start(f32[5,32,128]{2,1,0:T(8,128)S(1)} %bitcast.75), channel_id=1, source_target_pairs={{0,8},{4,12},{1,9},{5,13},{2,10},{6,14},{3,11},{7,15},{16,24},{20,... | collective-permute-start | bytes 245768 | tf_op jit(solution)/shard_map/ppermute | solution.py:67
  119.9 2.0 %collective-permute-done.15 = f32[5,32,128]{2,1,0:T(8,128)S(1)} collective-permute-done((f32[5,32,128]{2,1,0:T(8,128)S(1)}, f32[5,32,128]{2,1,0:T(8,128)S(1)}, u32[]{:S(2)}, u32[]{:S(2)}) %collective-permute-start.15) | collective-permute-done | bytes 81952 | tf_op jit(solution)/shard_map/ppermute | solution.py:67
  121.9 0.1 multiply_add_fusion.10
  122.0 5.9 %fusion.19 = f32[5,32,64,128]{3,2,1,0:T(8,128)S(1)} fusion(f32[5,32,64,128]{3,2,1,0:T(8,128)S(1)} %fusion.16, f32[5,32,128]{2,1,0:T(8,128)S(1)} %multiply_add_fusion.10, f32[5,64]{1,0:T(8,128)S(1)} %get-tuple-element.88, f32[5,64]{1,0:T(8,128)S(1)} %get-tuple-element.74, f32[5,64]{1,0:T(8,128)S(1)} %fusion.85, pred[64,64]{1,0:T(8,128)(4,1)S(1)} %iota_compare_fusion), kind=kOutput, calls=%fused_computation.20 | convolution fusion | flops 1009315840 | bytes 10575616 | tf_op jit(solution)/shard_map/fik,fxkz->fxiz/dot_general | solution.py:99
  127.9 0.1 slice.55
  128.0 1.3 collective-permute-start.19
  129.3 1.3 collective-permute-start.17
  130.6 1.3 collective-permute-start.18
  131.9 3.6 %collective-permute-done.19 = f32[5,32,128]{2,1,0:T(8,128)S(1)} collective-permute-done((f32[5,32,128]{2,1,0:T(8,128)S(1)}, f32[5,32,128]{2,1,0:T(8,128)S(1)}, u32[]{:S(2)}, u32[]{:S(2)}) %collective-permute-start.19) | collective-permute-done | bytes 81952 | tf_op jit(solution)/shard_map/ppermute | solution.py:67
  135.5 0.1 collective-permute-done.17
  135.6 2.8 %collective-permute-done.18 = f32[5,32,128]{2,1,0:T(8,128)S(1)} collective-permute-done((f32[5,32,128]{2,1,0:T(8,128)S(1)}, f32[5,32,128]{2,1,0:T(8,128)S(1)}, u32[]{:S(2)}, u32[]{:S(2)}) %collective-permute-start.18) | collective-permute-done | bytes 81952 | tf_op jit(solution)/shard_map/ppermute | solution.py:67
  138.4 0.1 multiply_add_fusion.9
  138.5 3.3 %multiply_add_fusion = f32[5,32,64,128]{3,2,1,0:T(8,128)} fusion(f32[5,32,64,128]{3,2,1,0:T(8,128)S(1)} %fusion.19, f32[5,32,128]{2,1,0:T(8,128)S(1)} %multiply_add_fusion.9, f32[5,64]{1,0:T(8,128)S(1)} %get-tuple-element.73), kind=kLoop, calls=%fused_computation | loop fusion | flops 2621440 | bytes 10568960 | tf_op jit(solution)/shard_map/add | solution.py:102
  (32 shorter events, 0.3 us)
Async XLA Ops:
  1.1 10.1 %collective-permute-start = (f32[5,2,64,128]{3,2,1,0:T(8,128)S(1)}, f32[5,2,64,128]{3,2,1,0:T(8,128)S(1)}, u32[]{:S(2)}, u32[]{:S(2)}) collective-permute-start(f32[5,2,64,128]{3,2,1,0:T(8,128)S(1)} %get-tuple-element.82), channel_id=1, source_target_pairs={{0,16},{16,32},{32,48},{48,64},{64,80},{80,96},{96,112},{112,128},... | collective-permute-start | bytes 983048 | tf_op jit(solution)/shard_map/ppermute | solution.py:107
  1.1 10.0 %collective-permute-start.1 = (f32[5,2,64,128]{3,2,1,0:T(8,128)S(1)}, f32[5,2,64,128]{3,2,1,0:T(8,128)S(1)}, u32[]{:S(2)}, u32[]{:S(2)}) collective-permute-start(f32[5,2,64,128]{3,2,1,0:T(8,128)S(1)} %get-tuple-element.81), channel_id=1, source_target_pairs={{0,240},{16,0},{32,16},{48,32},{64,48},{80,64},{96,80},{112,96},{1... | collective-permute-start | bytes 983048 | tf_op jit(solution)/shard_map/ppermute | solution.py:107
  11.2 0.7 copy-start
  11.9 0.7 copy-start.1
  21.7 32.2 %collective-permute-start.4 = (f32[5,64,128]{2,1,0:T(8,128)S(1)}, f32[5,64,128]{2,1,0:T(8,128)S(1)}, u32[]{:S(2)}, u32[]{:S(2)}) collective-permute-start(f32[5,64,128]{2,1,0:T(8,128)S(1)} %slice_bitcast_fusion), channel_id=1, source_target_pairs={{0,16},{16,32},{32,48},{48,64},{64,80},{80,96},{96,112},{112,128},... | collective-permute-start | bytes 491528 | tf_op jit(solution)/shard_map/ppermute | solution.py:107
  21.7 32.1 %collective-permute-start.5 = (f32[5,64,128]{2,1,0:T(8,128)S(1)}, f32[5,64,128]{2,1,0:T(8,128)S(1)}, u32[]{:S(2)}, u32[]{:S(2)}) collective-permute-start(f32[5,64,128]{2,1,0:T(8,128)S(1)} %slice_bitcast_fusion), channel_id=1, source_target_pairs={{0,32},{16,48},{32,64},{48,80},{64,96},{80,112},{96,128},{112,144}... | collective-permute-start | bytes 491528 | tf_op jit(solution)/shard_map/ppermute | solution.py:107
  22.7 31.1 %collective-permute-start.6 = (f32[5,64,128]{2,1,0:T(8,128)S(1)}, f32[5,64,128]{2,1,0:T(8,128)S(1)}, u32[]{:S(2)}, u32[]{:S(2)}) collective-permute-start(f32[5,64,128]{2,1,0:T(8,128)S(1)} %slice_bitcast_fusion.1), channel_id=1, source_target_pairs={{0,240},{16,0},{32,16},{48,32},{64,48},{80,64},{96,80},{112,96},{1... | collective-permute-start | bytes 491528 | tf_op jit(solution)/shard_map/ppermute | solution.py:107
  25.6 29.0 %collective-permute-start.7 = (f32[5,64,128]{2,1,0:T(8,128)S(1)}, f32[5,64,128]{2,1,0:T(8,128)S(1)}, u32[]{:S(2)}, u32[]{:S(2)}) collective-permute-start(f32[5,64,128]{2,1,0:T(8,128)S(1)} %slice_bitcast_fusion.1), channel_id=1, source_target_pairs={{0,224},{16,240},{32,0},{48,16},{64,32},{80,48},{96,64},{112,80},{... | collective-permute-start | bytes 491528 | tf_op jit(solution)/shard_map/ppermute | solution.py:107
  36.1 10.0 %slice-start = ((s8[5242880]{0:T(1024)(128)(4,1)}), s8[4194304]{0:T(1024)(128)(4,1)S(1)}, s32[]{:S(2)}) async-start(s8[5242880]{0:T(1024)(128)(4,1)} %bitcast.71), calls=%async_computation | async-start | bytes 8388608
  36.2 10.0 %slice-start.1 = ((s8[5242880]{0:T(1024)(128)(4,1)}), s8[1048576]{0:T(1024)(128)(4,1)S(1)}, s32[]{:S(2)}) async-start(s8[5242880]{0:T(1024)(128)(4,1)} %bitcast.71), calls=%async_computation.1 | async-start | bytes 2097152
  36.2 8.5 %collective-permute-start.2 = (f32[5,32,3,64]{3,2,1,0:T(4,128)S(1)}, f32[5,32,3,64]{3,2,1,0:T(4,128)S(1)}, u32[]{:S(2)}, u32[]{:S(2)}) collective-permute-start(f32[5,32,3,64]{3,2,1,0:T(4,128)S(1)} %get-tuple-element.84), channel_id=1, source_target_pairs={{0,1},{1,2},{2,3},{3,0},{4,5},{5,6},{6,7},{7,4},{8,9},{9,10},{10,1... | collective-permute-start | bytes 368648 | tf_op jit(solution)/shard_map/ppermute | solution.py:107
  44.7 9.1 %collective-permute-start.3 = (f32[5,32,3,64]{3,2,1,0:T(4,128)S(1)}, f32[5,32,3,64]{3,2,1,0:T(4,128)S(1)}, u32[]{:S(2)}, u32[]{:S(2)}) collective-permute-start(f32[5,32,3,64]{3,2,1,0:T(4,128)S(1)} %get-tuple-element.83), channel_id=1, source_target_pairs={{0,3},{1,0},{2,1},{3,2},{4,7},{5,4},{6,5},{7,6},{8,11},{9,8},{10,9... | collective-permute-start | bytes 368648 | tf_op jit(solution)/shard_map/ppermute | solution.py:107
  53.8 0.7 copy-start.2
  54.6 12.1 %collective-permute-start.8 = (f32[5,64,128]{2,1,0:T(8,128)S(1)}, f32[5,64,128]{2,1,0:T(8,128)S(1)}, u32[]{:S(2)}, u32[]{:S(2)}) collective-permute-start(f32[5,64,128]{2,1,0:T(8,128)S(1)} %multiply_add_fusion.8), channel_id=1, source_target_pairs={{0,32},{16,48},{32,64},{48,80},{64,96},{80,112},{96,128},{112,144}... | collective-permute-start | bytes 491528 | tf_op jit(solution)/shard_map/ppermute | solution.py:107
  54.7 12.0 %collective-permute-start.9 = (f32[5,64,128]{2,1,0:T(8,128)S(1)}, f32[5,64,128]{2,1,0:T(8,128)}, u32[]{:S(2)}, u32[]{:S(2)}) collective-permute-start(f32[5,64,128]{2,1,0:T(8,128)S(1)} %multiply_add_fusion.7), channel_id=1, source_target_pairs={{0,224},{16,240},{32,0},{48,16},{64,32},{80,48},{96,64},{112,80},{... | collective-permute-start | bytes 491528 | tf_op jit(solution)/shard_map/ppermute | solution.py:107
  67.7 16.3 %collective-permute-start.10 = (f32[5,64,128]{2,1,0:T(8,128)S(1)}, f32[5,64,128]{2,1,0:T(8,128)S(1)}, u32[]{:S(2)}, u32[]{:S(2)}) collective-permute-start(f32[5,64,128]{2,1,0:T(8,128)S(1)} %multiply_add_fusion.6), channel_id=1, source_target_pairs={{0,64},{16,80},{32,96},{48,112},{64,128},{80,144},{96,160},{112,17... | collective-permute-start | bytes 491528 | tf_op jit(solution)/shard_map/ppermute | solution.py:107
  70.3 13.7 %collective-permute-start.11 = (f32[5,64,128]{2,1,0:T(8,128)S(1)}, f32[5,64,128]{2,1,0:T(8,128)S(1)}, u32[]{:S(2)}, u32[]{:S(2)}) collective-permute-start(f32[5,64,128]{2,1,0:T(8,128)S(1)} %multiply_add_fusion.5), channel_id=1, source_target_pairs={{0,192},{16,208},{32,224},{48,240},{64,0},{80,16},{96,32},{112,48}... | collective-permute-start | bytes 491528 | tf_op jit(solution)/shard_map/ppermute | solution.py:107
  84.1 13.7 %collective-permute-start.12 = (f32[5,64,128]{2,1,0:T(8,128)S(1)}, f32[5,64,128]{2,1,0:T(8,128)S(1)}, u32[]{:S(2)}, u32[]{:S(2)}) collective-permute-start(f32[5,64,128]{2,1,0:T(8,128)S(1)} %multiply_add_fusion.4), channel_id=1, source_target_pairs={{0,128},{16,144},{32,160},{48,176},{64,192},{80,208},{96,224},{112... | collective-permute-start | bytes 491528 | tf_op jit(solution)/shard_map/ppermute | solution.py:107
  89.0 13.2 %collective-permute-start.13 = (f32[5,64,128]{2,1,0:T(8,128)S(1)}, f32[5,64,128]{2,1,0:T(8,128)S(1)}, u32[]{:S(2)}, u32[]{:S(2)}) collective-permute-start(f32[5,64,128]{2,1,0:T(8,128)S(1)} %multiply_add_fusion.3), channel_id=1, source_target_pairs={{0,128},{16,144},{32,160},{48,176},{64,192},{80,208},{96,224},{112... | collective-permute-start | bytes 491528 | tf_op jit(solution)/shard_map/ppermute | solution.py:107
  110.5 9.4 %collective-permute-start.16 = (f32[5,32,128]{2,1,0:T(8,128)S(1)}, f32[5,32,128]{2,1,0:T(8,128)S(1)}, u32[]{:S(2)}, u32[]{:S(2)}) collective-permute-start(f32[5,32,128]{2,1,0:T(8,128)S(1)} %bitcast.73), channel_id=1, source_target_pairs={{0,12},{1,13},{2,14},{3,15},{16,28},{17,29},{18,30},{19,31},{32,44... | collective-permute-start | bytes 245768 | tf_op jit(solution)/shard_map/ppermute | solution.py:67
  115.2 4.7 %collective-permute-start.14 = (f32[5,32,128]{2,1,0:T(8,128)S(1)}, f32[5,32,128]{2,1,0:T(8,128)S(1)}, u32[]{:S(2)}, u32[]{:S(2)}) collective-permute-start(f32[5,32,128]{2,1,0:T(8,128)S(1)} %bitcast.74), channel_id=1, source_target_pairs={{0,4},{4,8},{8,12},{1,5},{5,9},{9,13},{2,6},{6,10},{10,14},{3,7},{... | collective-permute-start | bytes 245768 | tf_op jit(solution)/shard_map/ppermute | solution.py:67
  116.5 5.4 %collective-permute-start.15 = (f32[5,32,128]{2,1,0:T(8,128)S(1)}, f32[5,32,128]{2,1,0:T(8,128)S(1)}, u32[]{:S(2)}, u32[]{:S(2)}) collective-permute-start(f32[5,32,128]{2,1,0:T(8,128)S(1)} %bitcast.75), channel_id=1, source_target_pairs={{0,8},{4,12},{1,9},{5,13},{2,10},{6,14},{3,11},{7,15},{16,24},{20,... | collective-permute-start | bytes 245768 | tf_op jit(solution)/shard_map/ppermute | solution.py:67
  128.0 7.5 %collective-permute-start.19 = (f32[5,32,128]{2,1,0:T(8,128)S(1)}, f32[5,32,128]{2,1,0:T(8,128)S(1)}, u32[]{:S(2)}, u32[]{:S(2)}) collective-permute-start(f32[5,32,128]{2,1,0:T(8,128)S(1)} %bitcast.76), channel_id=1, source_target_pairs={{12,0},{13,1},{14,2},{15,3},{28,16},{29,17},{30,18},{31,19},{44,32... | collective-permute-start | bytes 245768 | tf_op jit(solution)/shard_map/ppermute | solution.py:67
  129.3 6.3 %collective-permute-start.17 = (f32[5,32,128]{2,1,0:T(8,128)S(1)}, f32[5,32,128]{2,1,0:T(8,128)S(1)}, u32[]{:S(2)}, u32[]{:S(2)}) collective-permute-start(f32[5,32,128]{2,1,0:T(8,128)S(1)} %bitcast.77), channel_id=1, source_target_pairs={{4,0},{8,4},{12,8},{5,1},{9,5},{13,9},{6,2},{10,6},{14,10},{7,3},{... | collective-permute-start | bytes 245768 | tf_op jit(solution)/shard_map/ppermute | solution.py:67
  130.6 7.8 %collective-permute-start.18 = (f32[5,32,128]{2,1,0:T(8,128)S(1)}, f32[5,32,128]{2,1,0:T(8,128)S(1)}, u32[]{:S(2)}, u32[]{:S(2)}) collective-permute-start(f32[5,32,128]{2,1,0:T(8,128)S(1)} %bitcast.78), channel_id=1, source_target_pairs={{8,0},{12,4},{9,1},{13,5},{10,2},{14,6},{11,3},{15,7},{24,16},{28,... | collective-permute-start | bytes 245768 | tf_op jit(solution)/shard_map/ppermute | solution.py:67
where the time goes:
time: 144 us; the launch traced here: 142 us
  matrix products  42.6 us (30%)
  starting transfers between devices  38.6 us (27%)
  waiting for transfers between devices  28.6 us (20%)
  other arithmetic  18 us (12%)
  Pallas kernels  8.1 us (6%)
  local copies, waits for them, and re-layouts  5.67 us (4%)
    ppermute x14, starting transfers between devices, shifted_in(): lax.ppermute(array, axis, [(i, (i + shift) % peers) for i in range(peers)])  25.3 us
    ppermute x14, waiting for transfers between devices, shifted_in(): lax.ppermute(array, axis, [(i, (i + shift) % peers) for i in range(peers)])  20 us
    ppermute x6, starting transfers between devices, carried_over(): arrived = lax.ppermute(line, 'gy', pairs)  13.2 us
    dot_general x1, matrix products, span_halo_term(): return jnp.einsum('fxcy,cz->fxyz', stacked, weights, precision=highest)  12 us
    sub x1, other arithmetic, inner_part(): late - advect * late[0] * local - advect * late[2] * inner  8.81 us
    dot_general x1, matrix products, span_halos(): edges = jnp.einsum('cz,fxyz->fxcy', pick, fields, precision=highest)  8.67 us
    ppermute x6, waiting for transfers between devices, carried_over(): arrived = lax.ppermute(line, 'gy', pairs)  8.54 us
    dot_general x1, matrix products, wall_carries(): jnp.einsum('fik,fxkz->fxiz', forward_table, explicit, precision=highest)  8.15 us
  transfers between devices with their start and end apart: 20, of which 9 were waited for; matrix products, arithmetic and copies ran while one was open for 31% of the time, Pallas kernels for 0%

commit v1 on v0

--- a/solution.py
+++ b/solution.py
@@ -188,9 +188,9 @@
         state, left, right = lax.optimization_barrier((state, left, right))
         from_left = shifted_in(left, "gx", span)
         from_right = shifted_in(right, "gx", -span)
-        if tasks and span != spans[-1]:
+        if span == spans[0]:
             tasks.pop(0)(state)
-        elif span == spans[-1]:
+        if span == spans[-1]:
             while tasks:
                 tasks.pop(0)(state)
         state, from_left, from_right = lax.optimization_barrier((state, from_left, from_right))

time: 144 us -> 145 us (level)
  the two profiles are of different devices: /device:TPU:24 before, /device:TPU:82 now
where the time goes in v1:
time: 145 us; the launch traced here: 144 us
  matrix products  39.4 us (27%)
  waiting for transfers between devices  36.4 us (25%)
  starting transfers between devices  36.2 us (25%)
  other arithmetic  18 us (12%)
  Pallas kernels  8.1 us (6%)
  local copies, waits for them, and re-layouts  5.66 us (4%)
    ppermute x14, waiting for transfers between devices, shifted_in(): lax.ppermute(array, axis, [(i, (i + shift) % peers) for i in range(peers)])  27.9 us
    ppermute x14, starting transfers between devices, shifted_in(): lax.ppermute(array, axis, [(i, (i + shift) % peers) for i in range(peers)])  21.8 us
    ppermute x6, starting transfers between devices, carried_over(): arrived = lax.ppermute(line, 'gy', pairs)  14.4 us
    dot_general x1, matrix products, span_halo_term(): return jnp.einsum('fxcy,cz->fxyz', stacked, weights, precision=highest)  10.6 us
    sub x1, other arithmetic, inner_part(): late - advect * late[0] * local - advect * late[2] * inner  8.81 us
    dot_general x1, matrix products, span_halos(): edges = jnp.einsum('cz,fxyz->fxcy', pick, fields, precision=highest)  8.67 us
    ppermute x6, waiting for transfers between devices, carried_over(): arrived = lax.ppermute(line, 'gy', pairs)  8.51 us
    pallas_call x1, Pallas kernels, line_local(): pl.pallas_call(line_kernel, grid=(count,), in_specs=[block(length), block...  8.1 us
  transfers between devices with their start and end apart: 20, of which 8 were waited for; matrix products, arithmetic and copies ran while one was open for 29% of the time, Pallas kernels for 0%

profile of v1, /device:TPU:82, one launch (start us, length us, event | category | flops | bytes accessed | tf_op | source)
XLA Modules:
  0.0 144.0 jit_solution(1691207044157590778)
XLA Ops:
  0.0 1.1 fusion.135
  1.1 0.0 collective-permute-start
  1.1 1.7 %collective-permute-start.1 = (f32[5,2,64,128]{3,2,1,0:T(8,128)S(1)}, f32[5,2,64,128]{3,2,1,0:T(8,128)S(1)}, u32[]{:S(2)}, u32[]{:S(2)}) collective-permute-start(f32[5,2,64,128]{3,2,1,0:T(8,128)S(1)} %get-tuple-element.89), channel_id=1, source_target_pairs={{0,240},{16,0},{32,16},{48,32},{64,48},{80,64},{96,80},{112,96},{1... | collective-permute-start | bytes 983048 | tf_op jit(solution)/shard_map/ppermute | solution.py:107
  2.9 0.7 log-plus-one_multiply_fusion
  3.6 0.8 fusion.132
  4.4 0.2 reduce_window_sum.13
  4.7 0.2 slice_reduce_fusion
  4.9 0.1 iota_compare_fusion.2
  4.9 0.1 subtract_exponential_fusion
  5.0 0.1 select_add_fusion
  5.1 1.3 multiply_bitcast_fusion
  6.4 1.2 collective-permute-done.before_ref
  7.6 0.7 copy-done.1
  8.4 0.7 copy-done.2
  9.1 8.1 %shard_map.28 = (f32[5,32,64,128]{3,2,1,0:T(8,128)}, f32[5,2,64,128]{3,2,1,0:T(8,128)}) custom-call(f32[5,32,64,128]{3,2,1,0:T(8,128)} %fields_ref.1, f32[5,2,64,128]{3,2,1,0:T(8,128)} %copy-done.1, f32[5,2,64,128]{3,2,1,0:T(8,128)} %copy-done.2), custom_call_target="tpu_custom_call" | custom-call | flops 26214400 | bytes 10485760 | tf_op jit(solution)/shard_map/pallas_call | solution.py:140
  17.2 0.9 slice_bitcast_fusion
  18.1 1.3 collective-permute-start.4
  19.4 4.3 %collective-permute-start.5 = (f32[5,64,128]{2,1,0:T(8,128)S(1)}, f32[5,64,128]{2,1,0:T(8,128)S(1)}, u32[]{:S(2)}, u32[]{:S(2)}) collective-permute-start(f32[5,64,128]{2,1,0:T(8,128)S(1)} %slice_bitcast_fusion), channel_id=1, source_target_pairs={{0,32},{16,48},{32,64},{48,80},{64,96},{80,112},{96,128},{112,144}... | collective-permute-start | bytes 491528 | tf_op jit(solution)/shard_map/ppermute | solution.py:107
  23.8 0.9 slice_bitcast_fusion.1
  24.7 0.0 collective-permute-start.6
  24.7 0.1 collective-permute-start.7
  24.8 8.7 %convolution_bitcast_fusion = f32[5,32,6,64]{3,2,1,0:T(8,128)S(1)} fusion(f32[5,32,64,128]{3,2,1,0:T(8,128)} %fields_ref.1, pred[3,128]{1,0:T(4,128)(4,1)S(1)} %get-tuple-element.103, pred[3,128]{1,0:T(4,128)(4,1)S(1)} %get-tuple-element.104), kind=kOutput, calls=%fused_computation.21 | convolution fusion | flops 94372608 | bytes 5489408 | tf_op jit(solution)/shard_map/cz,fxyz->fxcy/dot_general | solution.py:32
  33.5 0.1 fusion.136
  33.6 0.0 slice-start
  33.7 0.0 slice-start.1
  33.7 1.4 collective-permute-start.2
  35.0 7.9 %fusion.45 = f32[5,32,64,128]{3,2,1,0:T(8,128)} fusion(f32[5,32,64,128]{3,2,1,0:T(8,128)} %fields_ref.1), kind=kOutput, calls=%fused_computation.60 | convolution fusion | flops 2013560832 | bytes 10485760 | tf_op jit(solution)/shard_map/fxyw,wz->fxyz/dot_general | solution.py:39
  42.9 0.9 collective-permute-done.2
  43.8 0.5 collective-permute-start.3
  44.3 1.3 multiply_bitcast_fusion.2
  45.5 7.5 %collective-permute-done.3 = f32[5,32,3,64]{3,2,1,0:T(4,128)S(1)} collective-permute-done((f32[5,32,3,64]{3,2,1,0:T(4,128)S(1)}, f32[5,32,3,64]{3,2,1,0:T(4,128)S(1)}, u32[]{:S(2)}, u32[]{:S(2)}) %collective-permute-start.3) | collective-permute-done | bytes 122912 | tf_op jit(solution)/shard_map/ppermute | solution.py:107
  53.0 0.0 collective-permute-done.5
  53.0 0.0 collective-permute-done.6
  53.0 0.7 copy-done
  53.8 0.0 collective-permute-done.7
  53.8 1.8 %collective-permute-start.8 = (f32[5,64,128]{2,1,0:T(8,128)S(1)}, f32[5,64,128]{2,1,0:T(8,128)S(1)}, u32[]{:S(2)}, u32[]{:S(2)}) collective-permute-start(f32[5,64,128]{2,1,0:T(8,128)S(1)} %multiply_add_fusion.8), channel_id=1, source_target_pairs={{0,32},{16,48},{32,64},{48,80},{64,96},{80,112},{96,128},{112,144}... | collective-permute-start | bytes 491528 | tf_op jit(solution)/shard_map/ppermute | solution.py:107
  55.6 0.3 collective-permute-start.9
  55.9 8.8 %multiply_subtract_fusion.1 = f32[5,32,64,128]{3,2,1,0:T(8,128)} fusion(f32[5,32,64,128]{3,2,1,0:T(8,128)} %fusion.45, f32[5,32,64,128]{3,2,1,0:T(8,128)S(1)} %bitcast.72, f32[5,32,64,128]{3,2,1,0:T(8,128)} %get-tuple-element.55, f32[32,64,128]{2,1,0:T(8,128)S(1)} %get-tuple-element.88, f32[32,64,128]{2,1,0:T(8,128)} %get-tuple-element.87), kind=kLoop, calls=%fused_computation.11 | loop fusion | flops 5242880 | bytes 23068672 | tf_op jit(solution)/shard_map/sub | solution.py:180
  64.7 0.0 collective-permute-done.8
  64.7 0.0 collective-permute-done.9
  64.8 0.9 multiply_add_fusion.5
  65.7 4.3 %collective-permute-start.10 = (f32[5,64,128]{2,1,0:T(8,128)S(1)}, f32[5,64,128]{2,1,0:T(8,128)S(1)}, u32[]{:S(2)}, u32[]{:S(2)}) collective-permute-start(f32[5,64,128]{2,1,0:T(8,128)S(1)} %multiply_add_fusion.6), channel_id=1, source_target_pairs={{0,64},{16,80},{32,96},{48,112},{64,128},{80,144},{96,160},{112,17... | collective-permute-start | bytes 491528 | tf_op jit(solution)/shard_map/ppermute | solution.py:107
  70.1 4.4 %collective-permute-done.10 = f32[5,64,128]{2,1,0:T(8,128)S(1)} collective-permute-done((f32[5,64,128]{2,1,0:T(8,128)S(1)}, f32[5,64,128]{2,1,0:T(8,128)S(1)}, u32[]{:S(2)}, u32[]{:S(2)}) %collective-permute-start.10) | collective-permute-done | bytes 163872 | tf_op jit(solution)/shard_map/ppermute | solution.py:107
  74.5 13.9 %collective-permute-done.11 = f32[5,64,128]{2,1,0:T(8,128)S(1)} collective-permute-done((f32[5,64,128]{2,1,0:T(8,128)S(1)}, f32[5,64,128]{2,1,0:T(8,128)S(1)}, u32[]{:S(2)}, u32[]{:S(2)}) %collective-permute-start.11) | collective-permute-done | bytes 163872 | tf_op jit(solution)/shard_map/ppermute | solution.py:107
  88.5 0.1 collective-permute-start.12
  88.6 5.9 %collective-permute-start.13 = (f32[5,64,128]{2,1,0:T(8,128)S(1)}, f32[5,64,128]{2,1,0:T(8,128)S(1)}, u32[]{:S(2)}, u32[]{:S(2)}) collective-permute-start(f32[5,64,128]{2,1,0:T(8,128)S(1)} %multiply_add_fusion.3), channel_id=1, source_target_pairs={{0,128},{16,144},{32,160},{48,176},{64,192},{80,208},{96,224},{112... | collective-permute-start | bytes 491528 | tf_op jit(solution)/shard_map/ppermute | solution.py:107
  94.5 10.6 %multiply_subtract_fusion = f32[5,32,64,128]{3,2,1,0:T(8,128)S(1)} fusion(f32[5,32,64,128]{3,2,1,0:T(8,128)} %multiply_subtract_fusion.1, f32[32,64,128]{2,1,0:T(8,128)S(1)} %get-tuple-element.88, f32[5,32,3,64]{3,2,1,0:T(4,128)} %copy-done, f32[5,32,3,64]{3,2,1,0:T(4,128)S(1)} %collective-permute-done.2, f32[3,128]{1,0:T(4,128)S(1)} %get-tuple-element.105, ...), kind=kOutput, calls=%fused_computation.10 | convolution fusion | flops 97055488 | bytes 11783168 | tf_op jit(solution)/shard_map/fxcy,cz->fxyz/dot_general | solution.py:49
  105.1 0.0 collective-permute-done.13
  105.1 6.3 %fusion.16 = f32[5,32,64,128]{3,2,1,0:T(8,128)S(1)} fusion(f32[5,32,64,128]{3,2,1,0:T(8,128)S(1)} %multiply_subtract_fusion, f32[32,64,128]{2,1,0:T(8,128)S(1)} %multiply_bitcast_fusion, f32[5,64,128]{2,1,0:T(8,128)S(1)} %multiply_add_fusion.1, f32[32]{0:T(128)S(1)} %get-tuple-element.108, f32[5,64,128]{2,1,0:T(8,128)S(1)} %multiply_add_fusion.2, ...), kind=kOutput, calls=%fused_computation.19 | convolution fusion | flops 1013268480 | bytes 11868928 | tf_op jit(solution)/shard_map/fik,fxkz->fxiz/dot_general | solution.py:94
  111.5 0.1 slice.54
  111.6 0.7 collective-permute-start.16
  112.2 3.6 %collective-permute-start.14 = (f32[5,32,128]{2,1,0:T(8,128)S(1)}, f32[5,32,128]{2,1,0:T(8,128)S(1)}, u32[]{:S(2)}, u32[]{:S(2)}) collective-permute-start(f32[5,32,128]{2,1,0:T(8,128)S(1)} %bitcast.74), channel_id=1, source_target_pairs={{0,4},{4,8},{8,12},{1,5},{5,9},{9,13},{2,6},{6,10},{10,14},{3,7},{... | collective-permute-start | bytes 245768 | tf_op jit(solution)/shard_map/ppermute | solution.py:67
  115.9 2.6 %collective-permute-start.15 = (f32[5,32,128]{2,1,0:T(8,128)S(1)}, f32[5,32,128]{2,1,0:T(8,128)S(1)}, u32[]{:S(2)}, u32[]{:S(2)}) collective-permute-start(f32[5,32,128]{2,1,0:T(8,128)S(1)} %bitcast.75), channel_id=1, source_target_pairs={{0,8},{4,12},{1,9},{5,13},{2,10},{6,14},{3,11},{7,15},{16,24},{20,... | collective-permute-start | bytes 245768 | tf_op jit(solution)/shard_map/ppermute | solution.py:67
  118.5 2.0 %collective-permute-done.14 = f32[5,32,128]{2,1,0:T(8,128)S(1)} collective-permute-done((f32[5,32,128]{2,1,0:T(8,128)S(1)}, f32[5,32,128]{2,1,0:T(8,128)S(1)}, u32[]{:S(2)}, u32[]{:S(2)}) %collective-permute-start.14) | collective-permute-done | bytes 81952 | tf_op jit(solution)/shard_map/ppermute | solution.py:67
  120.5 0.1 multiply_add_fusion.10
  120.6 5.9 %fusion.19 = f32[5,32,64,128]{3,2,1,0:T(8,128)S(1)} fusion(f32[5,32,64,128]{3,2,1,0:T(8,128)S(1)} %fusion.16, f32[5,32,128]{2,1,0:T(8,128)S(1)} %multiply_add_fusion.10, f32[5,64]{1,0:T(8,128)S(1)} %get-tuple-element.96, f32[5,64]{1,0:T(8,128)S(1)} %get-tuple-element.82, f32[5,64]{1,0:T(8,128)S(1)} %fusion.85, pred[64,64]{1,0:T(8,128)(4,1)S(1)} %iota_compare_fusion), kind=kOutput, calls=%fused_computation.20 | convolution fusion | flops 1009315840 | bytes 10575616 | tf_op jit(solution)/shard_map/fik,fxkz->fxiz/dot_general | solution.py:99
  126.5 0.1 slice.55
  126.6 0.7 collective-permute-start.19
  127.2 5.6 %collective-permute-start.17 = (f32[5,32,128]{2,1,0:T(8,128)S(1)}, f32[5,32,128]{2,1,0:T(8,128)S(1)}, u32[]{:S(2)}, u32[]{:S(2)}) collective-permute-start(f32[5,32,128]{2,1,0:T(8,128)S(1)} %bitcast.77), channel_id=1, source_target_pairs={{4,0},{8,4},{12,8},{5,1},{9,5},{13,9},{6,2},{10,6},{14,10},{7,3},{... | collective-permute-start | bytes 245768 | tf_op jit(solution)/shard_map/ppermute | solution.py:67
  132.8 1.3 collective-permute-start.18
  134.1 2.3 %collective-permute-done.17 = f32[5,32,128]{2,1,0:T(8,128)S(1)} collective-permute-done((f32[5,32,128]{2,1,0:T(8,128)S(1)}, f32[5,32,128]{2,1,0:T(8,128)S(1)}, u32[]{:S(2)}, u32[]{:S(2)}) %collective-permute-start.17) | collective-permute-done | bytes 81952 | tf_op jit(solution)/shard_map/ppermute | solution.py:67
  136.4 4.2 %collective-permute-done.18 = f32[5,32,128]{2,1,0:T(8,128)S(1)} collective-permute-done((f32[5,32,128]{2,1,0:T(8,128)S(1)}, f32[5,32,128]{2,1,0:T(8,128)S(1)}, u32[]{:S(2)}, u32[]{:S(2)}) %collective-permute-start.18) | collective-permute-done | bytes 81952 | tf_op jit(solution)/shard_map/ppermute | solution.py:67
  140.6 0.1 multiply_add_fusion.9
  140.7 3.3 %multiply_add_fusion = f32[5,32,64,128]{3,2,1,0:T(8,128)} fusion(f32[5,32,64,128]{3,2,1,0:T(8,128)S(1)} %fusion.19, f32[5,32,128]{2,1,0:T(8,128)S(1)} %multiply_add_fusion.9, f32[5,64]{1,0:T(8,128)S(1)} %get-tuple-element.81), kind=kLoop, calls=%fused_computation | loop fusion | flops 2621440 | bytes 10568960 | tf_op jit(solution)/shard_map/add | solution.py:102
  (32 shorter events, 0.3 us)
Async XLA Ops:
  1.1 6.5 %collective-permute-start = (f32[5,2,64,128]{3,2,1,0:T(8,128)S(1)}, f32[5,2,64,128]{3,2,1,0:T(8,128)S(1)}, u32[]{:S(2)}, u32[]{:S(2)}) collective-permute-start(f32[5,2,64,128]{3,2,1,0:T(8,128)S(1)} %get-tuple-element.90), channel_id=1, source_target_pairs={{0,16},{16,32},{32,48},{48,64},{64,80},{80,96},{96,112},{112,128},... | collective-permute-start | bytes 983048 | tf_op jit(solution)/shard_map/ppermute | solution.py:107
  1.1 6.5 %collective-permute-start.1 = (f32[5,2,64,128]{3,2,1,0:T(8,128)S(1)}, f32[5,2,64,128]{3,2,1,0:T(8,128)S(1)}, u32[]{:S(2)}, u32[]{:S(2)}) collective-permute-start(f32[5,2,64,128]{3,2,1,0:T(8,128)S(1)} %get-tuple-element.89), channel_id=1, source_target_pairs={{0,240},{16,0},{32,16},{48,32},{64,48},{80,64},{96,80},{112,96},{1... | collective-permute-start | bytes 983048 | tf_op jit(solution)/shard_map/ppermute | solution.py:107
  7.6 0.7 copy-start.1
  8.4 0.7 copy-start.2
  18.1 34.9 %collective-permute-start.4 = (f32[5,64,128]{2,1,0:T(8,128)S(1)}, f32[5,64,128]{2,1,0:T(8,128)S(1)}, u32[]{:S(2)}, u32[]{:S(2)}) collective-permute-start(f32[5,64,128]{2,1,0:T(8,128)S(1)} %slice_bitcast_fusion), channel_id=1, source_target_pairs={{0,16},{16,32},{32,48},{48,64},{64,80},{80,96},{96,112},{112,128},... | collective-permute-start | bytes 491528 | tf_op jit(solution)/shard_map/ppermute | solution.py:107
  19.4 33.6 %collective-permute-start.5 = (f32[5,64,128]{2,1,0:T(8,128)S(1)}, f32[5,64,128]{2,1,0:T(8,128)S(1)}, u32[]{:S(2)}, u32[]{:S(2)}) collective-permute-start(f32[5,64,128]{2,1,0:T(8,128)S(1)} %slice_bitcast_fusion), channel_id=1, source_target_pairs={{0,32},{16,48},{32,64},{48,80},{64,96},{80,112},{96,128},{112,144}... | collective-permute-start | bytes 491528 | tf_op jit(solution)/shard_map/ppermute | solution.py:107
  24.7 28.3 %collective-permute-start.6 = (f32[5,64,128]{2,1,0:T(8,128)S(1)}, f32[5,64,128]{2,1,0:T(8,128)S(1)}, u32[]{:S(2)}, u32[]{:S(2)}) collective-permute-start(f32[5,64,128]{2,1,0:T(8,128)S(1)} %slice_bitcast_fusion.1), channel_id=1, source_target_pairs={{0,240},{16,0},{32,16},{48,32},{64,48},{80,64},{96,80},{112,96},{1... | collective-permute-start | bytes 491528 | tf_op jit(solution)/shard_map/ppermute | solution.py:107
  24.7 29.0 %collective-permute-start.7 = (f32[5,64,128]{2,1,0:T(8,128)S(1)}, f32[5,64,128]{2,1,0:T(8,128)S(1)}, u32[]{:S(2)}, u32[]{:S(2)}) collective-permute-start(f32[5,64,128]{2,1,0:T(8,128)S(1)} %slice_bitcast_fusion.1), channel_id=1, source_target_pairs={{0,224},{16,240},{32,0},{48,16},{64,32},{80,48},{96,64},{112,80},{... | collective-permute-start | bytes 491528 | tf_op jit(solution)/shard_map/ppermute | solution.py:107
  33.6 10.6 %slice-start = ((s8[5242880]{0:T(1024)(128)(4,1)}), s8[4194304]{0:T(1024)(128)(4,1)S(1)}, s32[]{:S(2)}) async-start(s8[5242880]{0:T(1024)(128)(4,1)} %bitcast.71), calls=%async_computation | async-start | bytes 8388608
  33.7 10.6 %slice-start.1 = ((s8[5242880]{0:T(1024)(128)(4,1)}), s8[1048576]{0:T(1024)(128)(4,1)S(1)}, s32[]{:S(2)}) async-start(s8[5242880]{0:T(1024)(128)(4,1)} %bitcast.71), calls=%async_computation.1 | async-start | bytes 2097152
  33.7 10.1 %collective-permute-start.2 = (f32[5,32,3,64]{3,2,1,0:T(4,128)S(1)}, f32[5,32,3,64]{3,2,1,0:T(4,128)S(1)}, u32[]{:S(2)}, u32[]{:S(2)}) collective-permute-start(f32[5,32,3,64]{3,2,1,0:T(4,128)S(1)} %get-tuple-element.92), channel_id=1, source_target_pairs={{0,1},{1,2},{2,3},{3,0},{4,5},{5,6},{6,7},{7,4},{8,9},{9,10},{10,1... | collective-permute-start | bytes 368648 | tf_op jit(solution)/shard_map/ppermute | solution.py:107
  43.8 9.2 %collective-permute-start.3 = (f32[5,32,3,64]{3,2,1,0:T(4,128)S(1)}, f32[5,32,3,64]{3,2,1,0:T(4,128)S(1)}, u32[]{:S(2)}, u32[]{:S(2)}) collective-permute-start(f32[5,32,3,64]{3,2,1,0:T(4,128)S(1)} %get-tuple-element.91), channel_id=1, source_target_pairs={{0,3},{1,0},{2,1},{3,2},{4,7},{5,4},{6,5},{7,6},{8,11},{9,8},{10,9... | collective-permute-start | bytes 368648 | tf_op jit(solution)/shard_map/ppermute | solution.py:107
  53.0 0.7 copy-start
  53.8 10.9 %collective-permute-start.8 = (f32[5,64,128]{2,1,0:T(8,128)S(1)}, f32[5,64,128]{2,1,0:T(8,128)S(1)}, u32[]{:S(2)}, u32[]{:S(2)}) collective-permute-start(f32[5,64,128]{2,1,0:T(8,128)S(1)} %multiply_add_fusion.8), channel_id=1, source_target_pairs={{0,32},{16,48},{32,64},{48,80},{64,96},{80,112},{96,128},{112,144}... | collective-permute-start | bytes 491528 | tf_op jit(solution)/shard_map/ppermute | solution.py:107
  55.6 9.1 %collective-permute-start.9 = (f32[5,64,128]{2,1,0:T(8,128)S(1)}, f32[5,64,128]{2,1,0:T(8,128)}, u32[]{:S(2)}, u32[]{:S(2)}) collective-permute-start(f32[5,64,128]{2,1,0:T(8,128)S(1)} %multiply_add_fusion.7), channel_id=1, source_target_pairs={{0,224},{16,240},{32,0},{48,16},{64,32},{80,48},{96,64},{112,80},{... | collective-permute-start | bytes 491528 | tf_op jit(solution)/shard_map/ppermute | solution.py:107
  65.7 8.8 %collective-permute-start.10 = (f32[5,64,128]{2,1,0:T(8,128)S(1)}, f32[5,64,128]{2,1,0:T(8,128)S(1)}, u32[]{:S(2)}, u32[]{:S(2)}) collective-permute-start(f32[5,64,128]{2,1,0:T(8,128)S(1)} %multiply_add_fusion.6), channel_id=1, source_target_pairs={{0,64},{16,80},{32,96},{48,112},{64,128},{80,144},{96,160},{112,17... | collective-permute-start | bytes 491528 | tf_op jit(solution)/shard_map/ppermute | solution.py:107
  70.0 18.4 %collective-permute-start.11 = (f32[5,64,128]{2,1,0:T(8,128)S(1)}, f32[5,64,128]{2,1,0:T(8,128)S(1)}, u32[]{:S(2)}, u32[]{:S(2)}) collective-permute-start(f32[5,64,128]{2,1,0:T(8,128)S(1)} %multiply_add_fusion.5), channel_id=1, source_target_pairs={{0,192},{16,208},{32,224},{48,240},{64,0},{80,16},{96,32},{112,48}... | collective-permute-start | bytes 491528 | tf_op jit(solution)/shard_map/ppermute | solution.py:107
  88.5 16.6 %collective-permute-start.12 = (f32[5,64,128]{2,1,0:T(8,128)S(1)}, f32[5,64,128]{2,1,0:T(8,128)S(1)}, u32[]{:S(2)}, u32[]{:S(2)}) collective-permute-start(f32[5,64,128]{2,1,0:T(8,128)S(1)} %multiply_add_fusion.4), channel_id=1, source_target_pairs={{0,128},{16,144},{32,160},{48,176},{64,192},{80,208},{96,224},{112... | collective-permute-start | bytes 491528 | tf_op jit(solution)/shard_map/ppermute | solution.py:107
  88.6 16.5 %collective-permute-start.13 = (f32[5,64,128]{2,1,0:T(8,128)S(1)}, f32[5,64,128]{2,1,0:T(8,128)S(1)}, u32[]{:S(2)}, u32[]{:S(2)}) collective-permute-start(f32[5,64,128]{2,1,0:T(8,128)S(1)} %multiply_add_fusion.3), channel_id=1, source_target_pairs={{0,128},{16,144},{32,160},{48,176},{64,192},{80,208},{96,224},{112... | collective-permute-start | bytes 491528 | tf_op jit(solution)/shard_map/ppermute | solution.py:107
  111.6 6.9 %collective-permute-start.16 = (f32[5,32,128]{2,1,0:T(8,128)S(1)}, f32[5,32,128]{2,1,0:T(8,128)S(1)}, u32[]{:S(2)}, u32[]{:S(2)}) collective-permute-start(f32[5,32,128]{2,1,0:T(8,128)S(1)} %bitcast.73), channel_id=1, source_target_pairs={{0,12},{1,13},{2,14},{3,15},{16,28},{17,29},{18,30},{19,31},{32,44... | collective-permute-start | bytes 245768 | tf_op jit(solution)/shard_map/ppermute | solution.py:67
  112.2 8.2 %collective-permute-start.14 = (f32[5,32,128]{2,1,0:T(8,128)S(1)}, f32[5,32,128]{2,1,0:T(8,128)S(1)}, u32[]{:S(2)}, u32[]{:S(2)}) collective-permute-start(f32[5,32,128]{2,1,0:T(8,128)S(1)} %bitcast.74), channel_id=1, source_target_pairs={{0,4},{4,8},{8,12},{1,5},{5,9},{9,13},{2,6},{6,10},{10,14},{3,7},{... | collective-permute-start | bytes 245768 | tf_op jit(solution)/shard_map/ppermute | solution.py:67
  115.9 4.6 %collective-permute-start.15 = (f32[5,32,128]{2,1,0:T(8,128)S(1)}, f32[5,32,128]{2,1,0:T(8,128)S(1)}, u32[]{:S(2)}, u32[]{:S(2)}) collective-permute-start(f32[5,32,128]{2,1,0:T(8,128)S(1)} %bitcast.75), channel_id=1, source_target_pairs={{0,8},{4,12},{1,9},{5,13},{2,10},{6,14},{3,11},{7,15},{16,24},{20,... | collective-permute-start | bytes 245768 | tf_op jit(solution)/shard_map/ppermute | solution.py:67
  126.6 7.5 %collective-permute-start.19 = (f32[5,32,128]{2,1,0:T(8,128)S(1)}, f32[5,32,128]{2,1,0:T(8,128)S(1)}, u32[]{:S(2)}, u32[]{:S(2)}) collective-permute-start(f32[5,32,128]{2,1,0:T(8,128)S(1)} %bitcast.76), channel_id=1, source_target_pairs={{12,0},{13,1},{14,2},{15,3},{28,16},{29,17},{30,18},{31,19},{44,32... | collective-permute-start | bytes 245768 | tf_op jit(solution)/shard_map/ppermute | solution.py:67
  127.2 9.2 %collective-permute-start.17 = (f32[5,32,128]{2,1,0:T(8,128)S(1)}, f32[5,32,128]{2,1,0:T(8,128)S(1)}, u32[]{:S(2)}, u32[]{:S(2)}) collective-permute-start(f32[5,32,128]{2,1,0:T(8,128)S(1)} %bitcast.77), channel_id=1, source_target_pairs={{4,0},{8,4},{12,8},{5,1},{9,5},{13,9},{6,2},{10,6},{14,10},{7,3},{... | collective-permute-start | bytes 245768 | tf_op jit(solution)/shard_map/ppermute | solution.py:67
  132.8 7.8 %collective-permute-start.18 = (f32[5,32,128]{2,1,0:T(8,128)S(1)}, f32[5,32,128]{2,1,0:T(8,128)S(1)}, u32[]{:S(2)}, u32[]{:S(2)}) collective-permute-start(f32[5,32,128]{2,1,0:T(8,128)S(1)} %bitcast.78), channel_id=1, source_target_pairs={{8,0},{12,4},{9,1},{13,5},{10,2},{14,6},{11,3},{15,7},{24,16},{28,... | collective-permute-start | bytes 245768 | tf_op jit(solution)/shard_map/ppermute | solution.py:67

commit v2 on v0

--- a/solution.py
+++ b/solution.py
@@ -22,16 +22,8 @@
     return sum((w / 60.0) * (offset == k).astype(jnp.float32) for k, w in weights.items())
 
 
-def span_halos(fields):
-    cols = fields.shape[3]
-    lanes = jnp.arange(cols)
-    halo = jnp.arange(3)
-    pick = jnp.concatenate(
-        [lanes[None, :] == cols - 3 + halo[:, None], lanes[None, :] == halo[:, None]]
-    ).astype(jnp.float32)
-    edges = jnp.einsum("cz,fxyz->fxcy", pick, fields, precision=highest)
-    return shifted_in(edges[:, :, :3], "gz", 1), shifted_in(edges[:, :, 3:], "gz", -1)
-
+def span_halos(edges):
+    return shifted_in(edges[:, :, :3], "gz", 1), shifted_in(edges[:, :, 3:6], "gz", -1)
 
 def span_inner(fields):
     lanes = jnp.arange(fields.shape[3])
@@ -107,8 +99,13 @@
     return lax.ppermute(array, axis, [(i, (i + shift) % peers) for i in range(peers)])
 
 
-def line_kernel(fields_ref, before_ref, after_ref, local_ref, moments_ref):
+def line_kernel(fields_ref, before_ref, after_ref, pick_ref, local_ref, moments_ref, edges_ref):
     length = fields_ref.shape[1]
+    for i in range(length):
+        edges_ref[0, i] = lax.dot_general(
+            pick_ref[...], fields_ref[0, i], (((1,), (1,)), ((), ())),
+            precision=highest, preferred_element_type=jnp.float32,
+        )
 
     def plane(k):
         if k < 0:
@@ -136,19 +133,24 @@
 def line_local(fields, before, after):
     count, length, rows, cols = fields.shape
     block = lambda depth: pl.BlockSpec((1, depth, rows, cols), lambda f: (f, 0, 0, 0))
+    lanes = jnp.arange(cols)
+    halo = jnp.arange(8)
+    pick = ((lanes[None, :] == cols - 3 + halo[:, None]) & (halo[:, None] < 3)) | (
+        (lanes[None, :] == halo[:, None] - 3) & (halo[:, None] >= 3) & (halo[:, None] < 6)
+    )
     size = fields.size * 4
     return pl.pallas_call(
         line_kernel,
         grid=(count,),
-        in_specs=[block(length), block(2), block(2)],
-        out_specs=[block(length), block(2)],
+        in_specs=[block(length), block(2), block(2), pl.BlockSpec((8, cols), lambda f: (0, 0))],
+        out_specs=[block(length), block(2), pl.BlockSpec((1, length, 8, rows), lambda f: (f, 0, 0, 0))],
         out_shape=[
             jax.ShapeDtypeStruct(fields.shape, jnp.float32),
             jax.ShapeDtypeStruct((count, 2, rows, cols), jnp.float32),
+            jax.ShapeDtypeStruct((count, length, 8, rows), jnp.float32),
         ],
         cost_estimate=pl.CostEstimate(flops=20 * fields.size, bytes_accessed=2 * size, transcendentals=0),
-    )(fields, before, after)
-
+    )(fields, before, after, pick.astype(jnp.float32))
 
 def shards(fields, viscous):
     length = fields.shape[1]
@@ -156,7 +158,7 @@
     total = length * peers
     before = shifted_in(fields[:, length - 2 :], "gx", 1)
     after = shifted_in(fields[:, :2], "gx", -1)
-    local, moments = line_local(fields, before, after)
+    local, moments, edges = line_local(fields, before, after)
     late, local, moments = lax.optimization_barrier((fields, local, moments))
     block_weight = root_ratio**length
     arrived = (
@@ -165,7 +167,7 @@
         shifted_in(moments[:, 1], "gx", -1),
         shifted_in(moments[:, 1], "gx", -2),
     )
-    state = {"halos": span_halos(late)}
+    state = {"halos": span_halos(edges)}
     state, arrived = lax.optimization_barrier((state, arrived))
     left = arrived[0] + block_weight * arrived[1]
     right = arrived[2] + block_weight * arrived[3]

time: 144 us -> 141 us (0.979)
  matrix products: 42.6 us -> 34 us
  Pallas kernels: 8.1 us -> 13.5 us
    dot_general x1 -> x0, matrix products: 8.67 us -> none  [span_halos(): edges = jnp.einsum('cz,fxyz->fxcy', pick, fields, precision=highest)]
    pallas_call x1, Pallas kernels: 8.1 us -> 13.5 us  [line_local(): pl.pallas_call(line_kernel, grid=(count,), in_specs=[block(length), block...]
  transfers between devices with their start and end apart: 20 -> 20, of which waited for: 9 -> 9; matrix products, arithmetic and copies ran while one was open for 31% -> 26% of each run, Pallas kernels for 0% -> 0%
where the time goes in v2:
time: 141 us; the launch traced here: 140 us
  starting transfers between devices  38.6 us (27%)
  matrix products  34 us (24%)
  waiting for transfers between devices  27.9 us (20%)
  other arithmetic  18.6 us (13%)
  Pallas kernels  13.5 us (10%)
  local copies, waits for them, and re-layouts  6.91 us (5%)
    ppermute x14, starting transfers between devices, shifted_in(): lax.ppermute(array, axis, [(i, (i + shift) % peers) for i in range(peers)])  25.4 us
    ppermute x14, waiting for transfers between devices, shifted_in(): lax.ppermute(array, axis, [(i, (i + shift) % peers) for i in range(peers)])  19.4 us
    pallas_call x1, Pallas kernels, line_local(): pl.pallas_call(line_kernel, grid=(count,), in_specs=[block(length), block...  13.5 us
    ppermute x6, starting transfers between devices, carried_over(): arrived = lax.ppermute(line, 'gy', pairs)  13.2 us
    dot_general x1, matrix products, span_halo_term(): return jnp.einsum('fxcy,cz->fxyz', stacked, weights, precision=highest)  12 us
    sub x1, other arithmetic, inner_part(): late - advect * late[0] * local - advect * late[2] * inner  8.81 us
    ppermute x6, waiting for transfers between devices, carried_over(): arrived = lax.ppermute(line, 'gy', pairs)  8.54 us
    dot_general x1, matrix products, wall_carries(): jnp.einsum('fik,fxkz->fxiz', forward_table, explicit, precision=highest)  8.15 us
  transfers between devices with their start and end apart: 20, of which 9 were waited for; matrix products, arithmetic and copies ran while one was open for 26% of the time, Pallas kernels for 0%

profile of v2, /device:TPU:24, one launch (start us, length us, event | category | flops | bytes accessed | tf_op | source)
XLA Modules:
  0.0 139.8 jit_solution(1227593088933319530)
XLA Ops:
  0.0 1.1 fusion.137
  1.1 0.0 collective-permute-start
  1.1 5.3 %collective-permute-start.1 = (f32[5,2,64,128]{3,2,1,0:T(8,128)S(1)}, f32[5,2,64,128]{3,2,1,0:T(8,128)S(1)}, u32[]{:S(2)}, u32[]{:S(2)}) collective-permute-start(f32[5,2,64,128]{3,2,1,0:T(8,128)S(1)} %get-tuple-element.83), channel_id=1, source_target_pairs={{0,240},{16,0},{32,16},{48,32},{64,48},{80,64},{96,80},{112,96},{1... | collective-permute-start | bytes 983048 | tf_op jit(solution)/shard_map/ppermute | solution.py:99
  6.5 0.7 log-plus-one_multiply_fusion
  7.2 0.8 fusion.134
  8.0 0.2 reduce_window_sum.13
  8.3 0.2 slice_reduce_fusion
  8.5 0.1 subtract_exponential_fusion
  8.5 0.1 select_add_fusion
  8.6 0.7 fusion.88.pick_ref
  9.3 1.3 multiply_bitcast_fusion
  10.6 0.6 collective-permute-done.before_ref
  11.2 0.7 copy-done
  11.9 0.7 copy-done.1
  12.6 13.5 %shard_map.28 = (f32[5,32,64,128]{3,2,1,0:T(8,128)}, f32[5,2,64,128]{3,2,1,0:T(8,128)}, f32[5,32,8,64]{3,2,1,0:T(8,128)}) custom-call(f32[5,32,64,128]{3,2,1,0:T(8,128)} %fields_ref.1, f32[5,2,64,128]{3,2,1,0:T(8,128)} %copy-done, f32[5,2,64,128]{3,2,1,0:T(8,128)} %copy-done.1, f32[8,128]{1,0:T(8,128)} %fusion.88.pick_ref), custom_call_target="tpu_custom_call" | custom-call | flops 26214400 | bytes 10485760 | tf_op jit(solution)/shard_map/pallas_call | solution.py:142
  26.2 0.9 slice_bitcast_fusion
  27.1 0.0 collective-permute-start.4
  27.1 0.1 collective-permute-start.5
  27.2 0.9 slice_bitcast_fusion.1
  28.1 2.9 %collective-permute-start.6 = (f32[5,64,128]{2,1,0:T(8,128)S(1)}, f32[5,64,128]{2,1,0:T(8,128)S(1)}, u32[]{:S(2)}, u32[]{:S(2)}) collective-permute-start(f32[5,64,128]{2,1,0:T(8,128)S(1)} %slice_bitcast_fusion.1), channel_id=1, source_target_pairs={{0,240},{16,0},{32,16},{48,32},{64,48},{80,64},{96,80},{112,96},{1... | collective-permute-start | bytes 491528 | tf_op jit(solution)/shard_map/ppermute | solution.py:99
  31.0 1.7 %collective-permute-start.7 = (f32[5,64,128]{2,1,0:T(8,128)S(1)}, f32[5,64,128]{2,1,0:T(8,128)S(1)}, u32[]{:S(2)}, u32[]{:S(2)}) collective-permute-start(f32[5,64,128]{2,1,0:T(8,128)S(1)} %slice_bitcast_fusion.1), channel_id=1, source_target_pairs={{0,224},{16,240},{32,0},{48,16},{64,32},{80,48},{96,64},{112,80},{... | collective-permute-start | bytes 491528 | tf_op jit(solution)/shard_map/ppermute | solution.py:99
  32.7 1.4 %fusion.138 = (f32[5,32,3,64]{3,2,1,0:T(4,128)S(1)}, f32[5,32,3,64]{3,2,1,0:T(4,128)S(1)}) fusion(f32[5,32,8,64]{3,2,1,0:T(8,128)} %get-tuple-element.40), kind=kLoop, calls=%fused_computation.181 | loop fusion | bytes 491520 | tf_op jit(solution)/shard_map/slice | solution.py:26
  34.1 0.0 slice-start
  34.2 0.3 collective-permute-start.2
  34.5 7.9 %fusion.45 = f32[5,32,64,128]{3,2,1,0:T(8,128)} fusion(f32[5,32,64,128]{3,2,1,0:T(8,128)} %fields_ref.1), kind=kOutput, calls=%fused_computation.59 | convolution fusion | flops 2013560832 | bytes 10485760 | tf_op jit(solution)/shard_map/fxyw,wz->fxyz/dot_general | solution.py:31
  42.4 0.4 collective-permute-done.2
  42.7 1.5 %collective-permute-start.3 = (f32[5,32,3,64]{3,2,1,0:T(4,128)S(1)}, f32[5,32,3,64]{3,2,1,0:T(4,128)S(1)}, u32[]{:S(2)}, u32[]{:S(2)}) collective-permute-start(f32[5,32,3,64]{3,2,1,0:T(4,128)S(1)} %get-tuple-element.85), channel_id=1, source_target_pairs={{0,3},{1,0},{2,1},{3,2},{4,7},{5,4},{6,5},{7,6},{8,11},{9,8},{10,9... | collective-permute-start | bytes 368648 | tf_op jit(solution)/shard_map/ppermute | solution.py:99
  44.2 1.3 multiply_bitcast_fusion.2
  45.5 6.4 %collective-permute-done.3 = f32[5,32,3,64]{3,2,1,0:T(4,128)S(1)} collective-permute-done((f32[5,32,3,64]{3,2,1,0:T(4,128)S(1)}, f32[5,32,3,64]{3,2,1,0:T(4,128)S(1)}, u32[]{:S(2)}, u32[]{:S(2)}) %collective-permute-start.3) | collective-permute-done | bytes 122912 | tf_op jit(solution)/shard_map/ppermute | solution.py:99
  51.8 0.0 collective-permute-done.6
  51.9 0.7 copy-done.2
  52.6 0.0 collective-permute-done.7
  52.6 0.1 collective-permute-start.8
  52.7 3.2 %collective-permute-start.9 = (f32[5,64,128]{2,1,0:T(8,128)S(1)}, f32[5,64,128]{2,1,0:T(8,128)}, u32[]{:S(2)}, u32[]{:S(2)}) collective-permute-start(f32[5,64,128]{2,1,0:T(8,128)S(1)} %multiply_add_fusion.7), channel_id=1, source_target_pairs={{0,224},{16,240},{32,0},{48,16},{64,32},{80,48},{96,64},{112,80},{... | collective-permute-start | bytes 491528 | tf_op jit(solution)/shard_map/ppermute | solution.py:99
  55.9 8.8 %multiply_subtract_fusion.1 = f32[5,32,64,128]{3,2,1,0:T(8,128)} fusion(f32[5,32,64,128]{3,2,1,0:T(8,128)} %fusion.45, f32[5,32,64,128]{3,2,1,0:T(8,128)S(1)} %bitcast.64, f32[5,32,64,128]{3,2,1,0:T(8,128)} %get-tuple-element.53, f32[32,64,128]{2,1,0:T(8,128)S(1)} %get-tuple-element.82, f32[32,64,128]{2,1,0:T(8,128)} %get-tuple-element.81), kind=kLoop, calls=%fused_computation.11 | loop fusion | flops 5242880 | bytes 23068672 | tf_op jit(solution)/shard_map/sub | solution.py:182
  64.7 0.0 collective-permute-done.8
  64.8 0.9 multiply_add_fusion.5
  65.7 2.5 %collective-permute-start.10 = (f32[5,64,128]{2,1,0:T(8,128)S(1)}, f32[5,64,128]{2,1,0:T(8,128)S(1)}, u32[]{:S(2)}, u32[]{:S(2)}) collective-permute-start(f32[5,64,128]{2,1,0:T(8,128)S(1)} %multiply_add_fusion.6), channel_id=1, source_target_pairs={{0,64},{16,80},{32,96},{48,112},{64,128},{80,144},{96,160},{112,17... | collective-permute-start | bytes 491528 | tf_op jit(solution)/shard_map/ppermute | solution.py:99
  68.3 1.7 %collective-permute-start.11 = (f32[5,64,128]{2,1,0:T(8,128)S(1)}, f32[5,64,128]{2,1,0:T(8,128)S(1)}, u32[]{:S(2)}, u32[]{:S(2)}) collective-permute-start(f32[5,64,128]{2,1,0:T(8,128)S(1)} %multiply_add_fusion.5), channel_id=1, source_target_pairs={{0,192},{16,208},{32,224},{48,240},{64,0},{80,16},{96,32},{112,48}... | collective-permute-start | bytes 491528 | tf_op jit(solution)/shard_map/ppermute | solution.py:99
  69.9 12.0 %multiply_subtract_fusion = f32[5,32,64,128]{3,2,1,0:T(8,128)} fusion(f32[5,32,64,128]{3,2,1,0:T(8,128)} %multiply_subtract_fusion.1, f32[32,64,128]{2,1,0:T(8,128)S(1)} %get-tuple-element.82, f32[5,32,3,64]{3,2,1,0:T(4,128)} %copy-done.2, f32[5,32,3,64]{3,2,1,0:T(4,128)S(1)} %collective-permute-done.2, f32[3,128]{1,0:T(4,128)S(1)} %get-tuple-element.101, ...), kind=kOutput, calls=%fused_computation.10 | convolution fusion | flops 97055488 | bytes 11783168 | tf_op jit(solution)/shard_map/fxcy,cz->fxyz/dot_general | solution.py:41
  82.0 0.0 collective-permute-done.10
  82.0 0.0 collective-permute-done.11
  82.1 4.9 %collective-permute-start.12 = (f32[5,64,128]{2,1,0:T(8,128)S(1)}, f32[5,64,128]{2,1,0:T(8,128)S(1)}, u32[]{:S(2)}, u32[]{:S(2)}) collective-permute-start(f32[5,64,128]{2,1,0:T(8,128)S(1)} %multiply_add_fusion.4), channel_id=1, source_target_pairs={{0,128},{16,144},{32,160},{48,176},{64,192},{80,208},{96,224},{112... | collective-permute-start | bytes 491528 | tf_op jit(solution)/shard_map/ppermute | solution.py:99
  87.0 1.1 collective-permute-start.13
  88.1 7.6 %collective-permute-done.12 = f32[5,64,128]{2,1,0:T(8,128)S(1)} collective-permute-done((f32[5,64,128]{2,1,0:T(8,128)S(1)}, f32[5,64,128]{2,1,0:T(8,128)S(1)}, u32[]{:S(2)}, u32[]{:S(2)}) %collective-permute-start.12) | collective-permute-done | bytes 163872 | tf_op jit(solution)/shard_map/ppermute | solution.py:99
  95.7 4.5 %collective-permute-done.13 = f32[5,64,128]{2,1,0:T(8,128)S(1)} collective-permute-done((f32[5,64,128]{2,1,0:T(8,128)S(1)}, f32[5,64,128]{2,1,0:T(8,128)S(1)}, u32[]{:S(2)}, u32[]{:S(2)}) %collective-permute-start.13) | collective-permute-done | bytes 163872 | tf_op jit(solution)/shard_map/ppermute | solution.py:99
  100.2 8.2 %fusion.16 = f32[5,32,64,128]{3,2,1,0:T(8,128)S(1)} fusion(f32[5,32,64,128]{3,2,1,0:T(8,128)} %multiply_subtract_fusion, f32[32,64,128]{2,1,0:T(8,128)S(1)} %multiply_bitcast_fusion, f32[5,64,128]{2,1,0:T(8,128)S(1)} %multiply_add_fusion.1, f32[32]{0:T(128)S(1)} %get-tuple-element.104, f32[5,64,128]{2,1,0:T(8,128)S(1)} %multiply_add_fusion.2, ...), kind=kOutput, calls=%fused_computation.19 | convolution fusion | flops 1013268480 | bytes 11868928 | tf_op jit(solution)/shard_map/fik,fxkz->fxiz/dot_general | solution.py:86
  108.4 0.1 slice.52
  108.5 4.7 %collective-permute-start.16 = (f32[5,32,128]{2,1,0:T(8,128)S(1)}, f32[5,32,128]{2,1,0:T(8,128)S(1)}, u32[]{:S(2)}, u32[]{:S(2)}) collective-permute-start(f32[5,32,128]{2,1,0:T(8,128)S(1)} %bitcast.65), channel_id=1, source_target_pairs={{0,12},{1,13},{2,14},{3,15},{16,28},{17,29},{18,30},{19,31},{32,44... | collective-permute-start | bytes 245768 | tf_op jit(solution)/shard_map/ppermute | solution.py:59
  113.2 1.3 collective-permute-start.14
  114.5 3.4 %collective-permute-start.15 = (f32[5,32,128]{2,1,0:T(8,128)S(1)}, f32[5,32,128]{2,1,0:T(8,128)S(1)}, u32[]{:S(2)}, u32[]{:S(2)}) collective-permute-start(f32[5,32,128]{2,1,0:T(8,128)S(1)} %bitcast.67), channel_id=1, source_target_pairs={{0,8},{4,12},{1,9},{5,13},{2,10},{6,14},{3,11},{7,15},{16,24},{20,... | collective-permute-start | bytes 245768 | tf_op jit(solution)/shard_map/ppermute | solution.py:59
  117.9 0.0 collective-permute-done.14
  117.9 2.0 %collective-permute-done.15 = f32[5,32,128]{2,1,0:T(8,128)S(1)} collective-permute-done((f32[5,32,128]{2,1,0:T(8,128)S(1)}, f32[5,32,128]{2,1,0:T(8,128)S(1)}, u32[]{:S(2)}, u32[]{:S(2)}) %collective-permute-start.15) | collective-permute-done | bytes 81952 | tf_op jit(solution)/shard_map/ppermute | solution.py:59
  119.9 0.1 multiply_add_fusion.10
  120.0 5.9 %fusion.19 = f32[5,32,64,128]{3,2,1,0:T(8,128)S(1)} fusion(f32[5,32,64,128]{3,2,1,0:T(8,128)S(1)} %fusion.16, f32[5,32,128]{2,1,0:T(8,128)S(1)} %multiply_add_fusion.10, f32[5,64]{1,0:T(8,128)S(1)} %get-tuple-element.90, f32[5,64]{1,0:T(8,128)S(1)} %get-tuple-element.76, f32[5,64]{1,0:T(8,128)S(1)} %fusion.85, pred[64,64]{1,0:T(8,128)(4,1)S(1)} %iota_compare_fusion), kind=kOutput, calls=%fused_computation.20 | convolution fusion | flops 1009315840 | bytes 10575616 | tf_op jit(solution)/shard_map/fik,fxkz->fxiz/dot_general | solution.py:91
  125.9 0.1 slice.53
  126.0 1.3 collective-permute-start.19
  127.3 1.3 collective-permute-start.17
  128.6 1.3 collective-permute-start.18
  129.9 3.6 %collective-permute-done.19 = f32[5,32,128]{2,1,0:T(8,128)S(1)} collective-permute-done((f32[5,32,128]{2,1,0:T(8,128)S(1)}, f32[5,32,128]{2,1,0:T(8,128)S(1)}, u32[]{:S(2)}, u32[]{:S(2)}) %collective-permute-start.19) | collective-permute-done | bytes 81952 | tf_op jit(solution)/shard_map/ppermute | solution.py:59
  133.5 0.1 collective-permute-done.17
  133.6 2.8 %collective-permute-done.18 = f32[5,32,128]{2,1,0:T(8,128)S(1)} collective-permute-done((f32[5,32,128]{2,1,0:T(8,128)S(1)}, f32[5,32,128]{2,1,0:T(8,128)S(1)}, u32[]{:S(2)}, u32[]{:S(2)}) %collective-permute-start.18) | collective-permute-done | bytes 81952 | tf_op jit(solution)/shard_map/ppermute | solution.py:59
  136.4 0.1 multiply_add_fusion.9
  136.5 3.3 %multiply_add_fusion = f32[5,32,64,128]{3,2,1,0:T(8,128)} fusion(f32[5,32,64,128]{3,2,1,0:T(8,128)S(1)} %fusion.19, f32[5,32,128]{2,1,0:T(8,128)S(1)} %multiply_add_fusion.9, f32[5,64]{1,0:T(8,128)S(1)} %get-tuple-element.75), kind=kLoop, calls=%fused_computation | loop fusion | flops 2621440 | bytes 10568960 | tf_op jit(solution)/shard_map/add | solution.py:94
  (33 shorter events, 0.3 us)
Async XLA Ops:
  1.1 10.1 %collective-permute-start = (f32[5,2,64,128]{3,2,1,0:T(8,128)S(1)}, f32[5,2,64,128]{3,2,1,0:T(8,128)S(1)}, u32[]{:S(2)}, u32[]{:S(2)}) collective-permute-start(f32[5,2,64,128]{3,2,1,0:T(8,128)S(1)} %get-tuple-element.84), channel_id=1, source_target_pairs={{0,16},{16,32},{32,48},{48,64},{64,80},{80,96},{96,112},{112,128},... | collective-permute-start | bytes 983048 | tf_op jit(solution)/shard_map/ppermute | solution.py:99
  1.1 10.0 %collective-permute-start.1 = (f32[5,2,64,128]{3,2,1,0:T(8,128)S(1)}, f32[5,2,64,128]{3,2,1,0:T(8,128)S(1)}, u32[]{:S(2)}, u32[]{:S(2)}) collective-permute-start(f32[5,2,64,128]{3,2,1,0:T(8,128)S(1)} %get-tuple-element.83), channel_id=1, source_target_pairs={{0,240},{16,0},{32,16},{48,32},{64,48},{80,64},{96,80},{112,96},{1... | collective-permute-start | bytes 983048 | tf_op jit(solution)/shard_map/ppermute | solution.py:99
  11.2 0.7 copy-start
  11.9 0.7 copy-start.1
  27.1 24.8 %collective-permute-start.4 = (f32[5,64,128]{2,1,0:T(8,128)S(1)}, f32[5,64,128]{2,1,0:T(8,128)S(1)}, u32[]{:S(2)}, u32[]{:S(2)}) collective-permute-start(f32[5,64,128]{2,1,0:T(8,128)S(1)} %slice_bitcast_fusion), channel_id=1, source_target_pairs={{0,16},{16,32},{32,48},{48,64},{64,80},{80,96},{96,112},{112,128},... | collective-permute-start | bytes 491528 | tf_op jit(solution)/shard_map/ppermute | solution.py:99
  27.1 24.7 %collective-permute-start.5 = (f32[5,64,128]{2,1,0:T(8,128)S(1)}, f32[5,64,128]{2,1,0:T(8,128)S(1)}, u32[]{:S(2)}, u32[]{:S(2)}) collective-permute-start(f32[5,64,128]{2,1,0:T(8,128)S(1)} %slice_bitcast_fusion), channel_id=1, source_target_pairs={{0,32},{16,48},{32,64},{48,80},{64,96},{80,112},{96,128},{112,144}... | collective-permute-start | bytes 491528 | tf_op jit(solution)/shard_map/ppermute | solution.py:99
  28.1 23.7 %collective-permute-start.6 = (f32[5,64,128]{2,1,0:T(8,128)S(1)}, f32[5,64,128]{2,1,0:T(8,128)S(1)}, u32[]{:S(2)}, u32[]{:S(2)}) collective-permute-start(f32[5,64,128]{2,1,0:T(8,128)S(1)} %slice_bitcast_fusion.1), channel_id=1, source_target_pairs={{0,240},{16,0},{32,16},{48,32},{64,48},{80,64},{96,80},{112,96},{1... | collective-permute-start | bytes 491528 | tf_op jit(solution)/shard_map/ppermute | solution.py:99
  31.0 21.6 %collective-permute-start.7 = (f32[5,64,128]{2,1,0:T(8,128)S(1)}, f32[5,64,128]{2,1,0:T(8,128)S(1)}, u32[]{:S(2)}, u32[]{:S(2)}) collective-permute-start(f32[5,64,128]{2,1,0:T(8,128)S(1)} %slice_bitcast_fusion.1), channel_id=1, source_target_pairs={{0,224},{16,240},{32,0},{48,16},{64,32},{80,48},{96,64},{112,80},{... | collective-permute-start | bytes 491528 | tf_op jit(solution)/shard_map/ppermute | solution.py:99
  34.1 10.1 %slice-start = ((s8[5242880]{0:T(1024)(128)(4,1)}), s8[4194304]{0:T(1024)(128)(4,1)S(1)}, s32[]{:S(2)}) async-start(s8[5242880]{0:T(1024)(128)(4,1)} %bitcast.63), calls=%async_computation | async-start | bytes 8388608
  34.2 10.0 %slice-start.1 = ((s8[5242880]{0:T(1024)(128)(4,1)}), s8[1048576]{0:T(1024)(128)(4,1)S(1)}, s32[]{:S(2)}) async-start(s8[5242880]{0:T(1024)(128)(4,1)} %bitcast.63), calls=%async_computation.1 | async-start | bytes 2097152
  34.2 8.5 %collective-permute-start.2 = (f32[5,32,3,64]{3,2,1,0:T(4,128)S(1)}, f32[5,32,3,64]{3,2,1,0:T(4,128)S(1)}, u32[]{:S(2)}, u32[]{:S(2)}) collective-permute-start(f32[5,32,3,64]{3,2,1,0:T(4,128)S(1)} %get-tuple-element.86), channel_id=1, source_target_pairs={{0,1},{1,2},{2,3},{3,0},{4,5},{5,6},{6,7},{7,4},{8,9},{9,10},{10,1... | collective-permute-start | bytes 368648 | tf_op jit(solution)/shard_map/ppermute | solution.py:99
  42.7 9.1 %collective-permute-start.3 = (f32[5,32,3,64]{3,2,1,0:T(4,128)S(1)}, f32[5,32,3,64]{3,2,1,0:T(4,128)S(1)}, u32[]{:S(2)}, u32[]{:S(2)}) collective-permute-start(f32[5,32,3,64]{3,2,1,0:T(4,128)S(1)} %get-tuple-element.85), channel_id=1, source_target_pairs={{0,3},{1,0},{2,1},{3,2},{4,7},{5,4},{6,5},{7,6},{8,11},{9,8},{10,9... | collective-permute-start | bytes 368648 | tf_op jit(solution)/shard_map/ppermute | solution.py:99
  51.8 0.7 copy-start.2
  52.6 12.1 %collective-permute-start.8 = (f32[5,64,128]{2,1,0:T(8,128)S(1)}, f32[5,64,128]{2,1,0:T(8,128)S(1)}, u32[]{:S(2)}, u32[]{:S(2)}) collective-permute-start(f32[5,64,128]{2,1,0:T(8,128)S(1)} %multiply_add_fusion.8), channel_id=1, source_target_pairs={{0,32},{16,48},{32,64},{48,80},{64,96},{80,112},{96,128},{112,144}... | collective-permute-start | bytes 491528 | tf_op jit(solution)/shard_map/ppermute | solution.py:99
  52.7 12.0 %collective-permute-start.9 = (f32[5,64,128]{2,1,0:T(8,128)S(1)}, f32[5,64,128]{2,1,0:T(8,128)}, u32[]{:S(2)}, u32[]{:S(2)}) collective-permute-start(f32[5,64,128]{2,1,0:T(8,128)S(1)} %multiply_add_fusion.7), channel_id=1, source_target_pairs={{0,224},{16,240},{32,0},{48,16},{64,32},{80,48},{96,64},{112,80},{... | collective-permute-start | bytes 491528 | tf_op jit(solution)/shard_map/ppermute | solution.py:99
  65.7 16.3 %collective-permute-start.10 = (f32[5,64,128]{2,1,0:T(8,128)S(1)}, f32[5,64,128]{2,1,0:T(8,128)S(1)}, u32[]{:S(2)}, u32[]{:S(2)}) collective-permute-start(f32[5,64,128]{2,1,0:T(8,128)S(1)} %multiply_add_fusion.6), channel_id=1, source_target_pairs={{0,64},{16,80},{32,96},{48,112},{64,128},{80,144},{96,160},{112,17... | collective-permute-start | bytes 491528 | tf_op jit(solution)/shard_map/ppermute | solution.py:99
  68.3 13.7 %collective-permute-start.11 = (f32[5,64,128]{2,1,0:T(8,128)S(1)}, f32[5,64,128]{2,1,0:T(8,128)S(1)}, u32[]{:S(2)}, u32[]{:S(2)}) collective-permute-start(f32[5,64,128]{2,1,0:T(8,128)S(1)} %multiply_add_fusion.5), channel_id=1, source_target_pairs={{0,192},{16,208},{32,224},{48,240},{64,0},{80,16},{96,32},{112,48}... | collective-permute-start | bytes 491528 | tf_op jit(solution)/shard_map/ppermute | solution.py:99
  82.1 13.7 %collective-permute-start.12 = (f32[5,64,128]{2,1,0:T(8,128)S(1)}, f32[5,64,128]{2,1,0:T(8,128)S(1)}, u32[]{:S(2)}, u32[]{:S(2)}) collective-permute-start(f32[5,64,128]{2,1,0:T(8,128)S(1)} %multiply_add_fusion.4), channel_id=1, source_target_pairs={{0,128},{16,144},{32,160},{48,176},{64,192},{80,208},{96,224},{112... | collective-permute-start | bytes 491528 | tf_op jit(solution)/shard_map/ppermute | solution.py:99
  87.0 13.2 %collective-permute-start.13 = (f32[5,64,128]{2,1,0:T(8,128)S(1)}, f32[5,64,128]{2,1,0:T(8,128)S(1)}, u32[]{:S(2)}, u32[]{:S(2)}) collective-permute-start(f32[5,64,128]{2,1,0:T(8,128)S(1)} %multiply_add_fusion.3), channel_id=1, source_target_pairs={{0,128},{16,144},{32,160},{48,176},{64,192},{80,208},{96,224},{112... | collective-permute-start | bytes 491528 | tf_op jit(solution)/shard_map/ppermute | solution.py:99
  108.5 9.4 %collective-permute-start.16 = (f32[5,32,128]{2,1,0:T(8,128)S(1)}, f32[5,32,128]{2,1,0:T(8,128)S(1)}, u32[]{:S(2)}, u32[]{:S(2)}) collective-permute-start(f32[5,32,128]{2,1,0:T(8,128)S(1)} %bitcast.65), channel_id=1, source_target_pairs={{0,12},{1,13},{2,14},{3,15},{16,28},{17,29},{18,30},{19,31},{32,44... | collective-permute-start | bytes 245768 | tf_op jit(solution)/shard_map/ppermute | solution.py:59
  113.2 4.7 %collective-permute-start.14 = (f32[5,32,128]{2,1,0:T(8,128)S(1)}, f32[5,32,128]{2,1,0:T(8,128)S(1)}, u32[]{:S(2)}, u32[]{:S(2)}) collective-permute-start(f32[5,32,128]{2,1,0:T(8,128)S(1)} %bitcast.66), channel_id=1, source_target_pairs={{0,4},{4,8},{8,12},{1,5},{5,9},{9,13},{2,6},{6,10},{10,14},{3,7},{... | collective-permute-start | bytes 245768 | tf_op jit(solution)/shard_map/ppermute | solution.py:59
  114.5 5.4 %collective-permute-start.15 = (f32[5,32,128]{2,1,0:T(8,128)S(1)}, f32[5,32,128]{2,1,0:T(8,128)S(1)}, u32[]{:S(2)}, u32[]{:S(2)}) collective-permute-start(f32[5,32,128]{2,1,0:T(8,128)S(1)} %bitcast.67), channel_id=1, source_target_pairs={{0,8},{4,12},{1,9},{5,13},{2,10},{6,14},{3,11},{7,15},{16,24},{20,... | collective-permute-start | bytes 245768 | tf_op jit(solution)/shard_map/ppermute | solution.py:59
  126.0 7.5 %collective-permute-start.19 = (f32[5,32,128]{2,1,0:T(8,128)S(1)}, f32[5,32,128]{2,1,0:T(8,128)S(1)}, u32[]{:S(2)}, u32[]{:S(2)}) collective-permute-start(f32[5,32,128]{2,1,0:T(8,128)S(1)} %bitcast.68), channel_id=1, source_target_pairs={{12,0},{13,1},{14,2},{15,3},{28,16},{29,17},{30,18},{31,19},{44,32... | collective-permute-start | bytes 245768 | tf_op jit(solution)/shard_map/ppermute | solution.py:59
  127.3 6.3 %collective-permute-start.17 = (f32[5,32,128]{2,1,0:T(8,128)S(1)}, f32[5,32,128]{2,1,0:T(8,128)S(1)}, u32[]{:S(2)}, u32[]{:S(2)}) collective-permute-start(f32[5,32,128]{2,1,0:T(8,128)S(1)} %bitcast.69), channel_id=1, source_target_pairs={{4,0},{8,4},{12,8},{5,1},{9,5},{13,9},{6,2},{10,6},{14,10},{7,3},{... | collective-permute-start | bytes 245768 | tf_op jit(solution)/shard_map/ppermute | solution.py:59
  128.6 7.8 %collective-permute-start.18 = (f32[5,32,128]{2,1,0:T(8,128)S(1)}, f32[5,32,128]{2,1,0:T(8,128)S(1)}, u32[]{:S(2)}, u32[]{:S(2)}) collective-permute-start(f32[5,32,128]{2,1,0:T(8,128)S(1)} %bitcast.70), channel_id=1, source_target_pairs={{8,0},{12,4},{9,1},{13,5},{10,2},{14,6},{11,3},{15,7},{24,16},{28,... | collective-permute-start | bytes 245768 | tf_op jit(solution)/shard_map/ppermute | solution.py:59

commit v3 on v2

--- a/solution.py
+++ b/solution.py
@@ -99,7 +99,7 @@
     return lax.ppermute(array, axis, [(i, (i + shift) % peers) for i in range(peers)])
 
 
-def line_kernel(fields_ref, before_ref, after_ref, pick_ref, local_ref, moments_ref, edges_ref):
+def line_kernel(fields_ref, before_ref, after_ref, pick_ref, along_ref, across_ref, inner_ref, local_ref, moments_ref, edges_ref):
     length = fields_ref.shape[1]
     for i in range(length):
         edges_ref[0, i] = lax.dot_general(
@@ -126,7 +126,10 @@
     for i in reversed(range(length)):
         value = source(i)
         running = value + root_ratio * running
-        local_ref[0, i] = line_gain * (local_ref[0, i] + running - value)
+        slope = line_gain * (local_ref[0, i] + running - value)
+        plain = fields_ref[0, i]
+        inner = jnp.dot(plain, inner_ref[...], precision=highest, preferred_element_type=jnp.float32)
+        local_ref[0, i] = plain - advect * along_ref[0, i] * slope - advect * across_ref[0, i] * inner
     moments_ref[0, 1] = running
 
 
@@ -142,7 +145,12 @@
     return pl.pallas_call(
         line_kernel,
         grid=(count,),
-        in_specs=[block(length), block(2), block(2), pl.BlockSpec((8, cols), lambda f: (0, 0))],
+        in_specs=[
+            block(length), block(2), block(2), pl.BlockSpec((8, cols), lambda f: (0, 0)),
+            pl.BlockSpec((1, length, rows, cols), lambda f: (0, 0, 0, 0)),
+            pl.BlockSpec((1, length, rows, cols), lambda f: (2, 0, 0, 0)),
+            pl.BlockSpec((cols, cols), lambda f: (0, 0)),
+        ],
         out_specs=[block(length), block(2), pl.BlockSpec((1, length, 8, rows), lambda f: (f, 0, 0, 0))],
         out_shape=[
             jax.ShapeDtypeStruct(fields.shape, jnp.float32),
@@ -150,7 +158,7 @@
             jax.ShapeDtypeStruct((count, length, 8, rows), jnp.float32),
         ],
         cost_estimate=pl.CostEstimate(flops=20 * fields.size, bytes_accessed=2 * size, transcendentals=0),
-    )(fields, before, after, pick.astype(jnp.float32))
+    )(fields, before, after, pick.astype(jnp.float32), fields, fields, span_weights(lanes[:, None] - lanes[None, :]))
 
 def shards(fields, viscous):
     length = fields.shape[1]
@@ -178,8 +186,7 @@
         span *= 2
 
     def inner_part(state):
-        inner = span_inner(late)
-        state["partial"] = late - advect * late[0] * local - advect * late[2] * inner
+        state["partial"] = local
 
     def halo_part(state):
         halo_term = span_halo_term(*state["halos"], late.shape[3])

time: 141 us -> 140 us (level)
  waiting for transfers between devices: 27.9 us -> 39.9 us
  matrix products: 34 us -> 24.1 us
  other arithmetic: 18.6 us -> 9.62 us
  Pallas kernels: 13.5 us -> 21.6 us
    ppermute x14, waiting for transfers between devices: 19.4 us -> 29.7 us  [shifted_in(): lax.ppermute(array, axis, [(i, (i + shift) % peers) for i in range(peers)])]
    sub x1 -> x0, other arithmetic: 8.81 us -> none  [inner_part(): late - advect * late[0] * local - advect * late[2] * inner]
    pallas_call x1, Pallas kernels: 13.5 us -> 21.6 us  [line_local(): pl.pallas_call(line_kernel, grid=(count,), in_specs=[block(length), block...]
    dot_general x1 -> x0, matrix products: 7.89 us -> none  [span_inner(): return jnp.einsum('fxyw,wz->fxyz', fields, interior, precision=highest)]
    dot_general x1, matrix products: 12 us -> 10.2 us  [span_halo_term(): return jnp.einsum('fxcy,cz->fxyz', stacked, weights, precision=highest)]
    ppermute x6, waiting for transfers between devices: 8.54 us -> 10.1 us  [carried_over(): arrived = lax.ppermute(line, 'gy', pairs)]
  transfers between devices with their start and end apart: 20 -> 20, of which waited for: 9 -> 11; matrix products, arithmetic and copies ran while one was open for 26% -> 14% of each run, Pallas kernels for 0% -> 0%
where the time goes in v3:
time: 140 us
  waiting for transfers between devices  39.9 us (28%)
  starting transfers between devices  38 us (27%)
  matrix products  24.1 us (17%)
  Pallas kernels  21.6 us (15%)
  other arithmetic  9.62 us (7%)
  local copies, waits for them, and re-layouts  6.65 us (5%)
    ppermute x14, waiting for transfers between devices, shifted_in(): lax.ppermute(array, axis, [(i, (i + shift) % peers) for i in range(peers)])  29.7 us
    ppermute x14, starting transfers between devices, shifted_in(): lax.ppermute(array, axis, [(i, (i + shift) % peers) for i in range(peers)])  24.6 us
    pallas_call x1, Pallas kernels, line_local(): pl.pallas_call(line_kernel, grid=(count,), in_specs=[block(length), block...  21.6 us
    ppermute x6, starting transfers between devices, carried_over(): arrived = lax.ppermute(line, 'gy', pairs)  13.4 us
    dot_general x1, matrix products, span_halo_term(): return jnp.einsum('fxcy,cz->fxyz', stacked, weights, precision=highest)  10.2 us
    ppermute x6, waiting for transfers between devices, carried_over(): arrived = lax.ppermute(line, 'gy', pairs)  10.1 us
    dot_general x1, matrix products, wall_carries(): jnp.einsum('fik,fxkz->fxiz', forward_table, explicit, precision=highest)  8.1 us
    dot_general x1, matrix products, wall_carries(): jnp.einsum('fik,fxkz->fxiz', backward_table, eliminated, precision=highest)  5.87 us
  transfers between devices with their start and end apart: 20, of which 11 were waited for; matrix products, arithmetic and copies ran while one was open for 14% of the time, Pallas kernels for 0%

profile of v3, /device:TPU:24, one launch (start us, length us, event | category | flops | bytes accessed | tf_op | source)
XLA Modules:
  0.0 140.1 jit_solution(14387881100755713002)
XLA Ops:
  0.0 1.1 fusion.92
  1.1 0.0 collective-permute-start
  1.1 5.3 %collective-permute-start.1 = (f32[5,2,64,128]{3,2,1,0:T(8,128)S(1)}, f32[5,2,64,128]{3,2,1,0:T(8,128)S(1)}, u32[]{:S(2)}, u32[]{:S(2)}) collective-permute-start(f32[5,2,64,128]{3,2,1,0:T(8,128)S(1)} %get-tuple-element.81), channel_id=1, source_target_pairs={{0,240},{16,0},{32,16},{48,32},{64,48},{80,64},{96,80},{112,96},{1... | collective-permute-start | bytes 983048 | tf_op jit(solution)/shard_map/ppermute | solution.py:99
  6.5 0.7 log-plus-one_multiply_fusion
  7.2 0.8 fusion.89
  8.0 0.2 reduce_window_sum.13
  8.3 0.2 slice_reduce_fusion
  8.4 0.1 subtract_exponential_fusion
  8.5 0.1 select_add_fusion.1
  8.6 0.7 fusion.56.pick_ref
  9.3 0.7 select_add_fusion.inner_ref
  9.9 1.3 multiply_bitcast_fusion
  11.3 0.0 collective-permute-done.before_ref
  11.3 0.0 collective-permute-done.1.after_ref
  11.3 0.7 copy-done.1
  12.0 0.7 copy-done.2
  12.7 21.6 %shard_map.28 = (f32[5,32,64,128]{3,2,1,0:T(8,128)}, f32[5,2,64,128]{3,2,1,0:T(8,128)}, f32[5,32,8,64]{3,2,1,0:T(8,128)}) custom-call(f32[5,32,64,128]{3,2,1,0:T(8,128)} %across_ref.1, f32[5,2,64,128]{3,2,1,0:T(8,128)} %copy-done.1, f32[5,2,64,128]{3,2,1,0:T(8,128)} %copy-done.2, f32[8,128]{1,0:T(8,128)} %fusion.56.pick_ref, f32[5,32,64,128]{3,2,1,0:T(8,128)} %across_ref.1, ...), custom_call_target="tpu_custom_call" | custom-call | flops 26214400 | bytes 10485760 | tf_op jit(solution)/shard_map/pallas_call | solution.py:145
  34.3 1.1 slice_bitcast_fusion
  35.4 0.0 collective-permute-start.4
  35.4 0.1 collective-permute-start.5
  35.5 1.7 %fusion.93 = (f32[5,32,3,64]{3,2,1,0:T(4,128)S(1)}, f32[5,32,3,64]{3,2,1,0:T(4,128)S(1)}) fusion(f32[5,32,8,64]{3,2,1,0:T(8,128)} %get-tuple-element.40), kind=kLoop, calls=%fused_computation.141 | loop fusion | bytes 491520 | tf_op jit(solution)/shard_map/slice | solution.py:26
  37.2 0.3 collective-permute-start.2
  37.5 0.9 slice_bitcast_fusion.1
  38.5 2.4 %collective-permute-start.6 = (f32[5,64,128]{2,1,0:T(8,128)S(1)}, f32[5,64,128]{2,1,0:T(8,128)S(1)}, u32[]{:S(2)}, u32[]{:S(2)}) collective-permute-start(f32[5,64,128]{2,1,0:T(8,128)S(1)} %slice_bitcast_fusion.1), channel_id=1, source_target_pairs={{0,240},{16,0},{32,16},{48,32},{64,48},{80,64},{96,80},{112,96},{1... | collective-permute-start | bytes 491528 | tf_op jit(solution)/shard_map/ppermute | solution.py:99
  40.8 1.7 %collective-permute-start.7 = (f32[5,64,128]{2,1,0:T(8,128)S(1)}, f32[5,64,128]{2,1,0:T(8,128)S(1)}, u32[]{:S(2)}, u32[]{:S(2)}) collective-permute-start(f32[5,64,128]{2,1,0:T(8,128)S(1)} %slice_bitcast_fusion.1), channel_id=1, source_target_pairs={{0,224},{16,240},{32,0},{48,16},{64,32},{80,48},{96,64},{112,80},{... | collective-permute-start | bytes 491528 | tf_op jit(solution)/shard_map/ppermute | solution.py:99
  42.6 4.0 %collective-permute-done.2 = f32[5,32,3,64]{3,2,1,0:T(4,128)S(1)} collective-permute-done((f32[5,32,3,64]{3,2,1,0:T(4,128)S(1)}, f32[5,32,3,64]{3,2,1,0:T(4,128)S(1)}, u32[]{:S(2)}, u32[]{:S(2)}) %collective-permute-start.2) | collective-permute-done | bytes 122912 | tf_op jit(solution)/shard_map/ppermute | solution.py:99
  46.6 0.7 collective-permute-start.3
  47.4 8.9 %collective-permute-done.3 = f32[5,32,3,64]{3,2,1,0:T(4,128)S(1)} collective-permute-done((f32[5,32,3,64]{3,2,1,0:T(4,128)S(1)}, f32[5,32,3,64]{3,2,1,0:T(4,128)S(1)}, u32[]{:S(2)}, u32[]{:S(2)}) %collective-permute-start.3) | collective-permute-done | bytes 122912 | tf_op jit(solution)/shard_map/ppermute | solution.py:99
  56.3 0.0 collective-permute-done.4
  56.3 0.0 collective-permute-done.5
  56.3 0.0 collective-permute-done.6
  56.4 2.8 %collective-permute-start.8 = (f32[5,64,128]{2,1,0:T(8,128)S(1)}, f32[5,64,128]{2,1,0:T(8,128)S(1)}, u32[]{:S(2)}, u32[]{:S(2)}) collective-permute-start(f32[5,64,128]{2,1,0:T(8,128)S(1)} %multiply_add_fusion.8), channel_id=1, source_target_pairs={{0,32},{16,48},{32,64},{48,80},{64,96},{80,112},{96,128},{112,144}... | collective-permute-start | bytes 491528 | tf_op jit(solution)/shard_map/ppermute | solution.py:99
  59.2 0.9 collective-permute-start.9
  60.1 1.3 multiply_bitcast_fusion.1
  61.4 1.9 %collective-permute-done.8 = f32[5,64,128]{2,1,0:T(8,128)S(1)} collective-permute-done((f32[5,64,128]{2,1,0:T(8,128)S(1)}, f32[5,64,128]{2,1,0:T(8,128)S(1)}, u32[]{:S(2)}, u32[]{:S(2)}) %collective-permute-start.8) | collective-permute-done | bytes 163872 | tf_op jit(solution)/shard_map/ppermute | solution.py:99
  63.3 3.5 %collective-permute-done.9 = f32[5,64,128]{2,1,0:T(8,128)S(1)} collective-permute-done((f32[5,64,128]{2,1,0:T(8,128)S(1)}, f32[5,64,128]{2,1,0:T(8,128)S(1)}, u32[]{:S(2)}, u32[]{:S(2)}) %collective-permute-start.9) | collective-permute-done | bytes 163872 | tf_op jit(solution)/shard_map/ppermute | solution.py:99
  66.9 1.6 %collective-permute-start.10 = (f32[5,64,128]{2,1,0:T(8,128)S(1)}, f32[5,64,128]{2,1,0:T(8,128)S(1)}, u32[]{:S(2)}, u32[]{:S(2)}) collective-permute-start(f32[5,64,128]{2,1,0:T(8,128)S(1)} %multiply_add_fusion.6), channel_id=1, source_target_pairs={{0,64},{16,80},{32,96},{48,112},{64,128},{80,144},{96,160},{112,17... | collective-permute-start | bytes 491528 | tf_op jit(solution)/shard_map/ppermute | solution.py:99
  68.5 2.6 %collective-permute-start.11 = (f32[5,64,128]{2,1,0:T(8,128)S(1)}, f32[5,64,128]{2,1,0:T(8,128)S(1)}, u32[]{:S(2)}, u32[]{:S(2)}) collective-permute-start(f32[5,64,128]{2,1,0:T(8,128)S(1)} %multiply_add_fusion.5), channel_id=1, source_target_pairs={{0,192},{16,208},{32,224},{48,240},{64,0},{80,16},{96,32},{112,48}... | collective-permute-start | bytes 491528 | tf_op jit(solution)/shard_map/ppermute | solution.py:99
  71.1 10.2 %multiply_subtract_fusion = f32[5,32,64,128]{3,2,1,0:T(8,128)} fusion(f32[5,32,64,128]{3,2,1,0:T(8,128)S(1)} %copy-done, f32[32,64,128]{2,1,0:T(8,128)S(1)} %multiply_bitcast_fusion.1, f32[5,32,3,64]{3,2,1,0:T(4,128)S(1)} %collective-permute-done.3, f32[5,32,3,64]{3,2,1,0:T(4,128)S(1)} %collective-permute-done.2, f32[3,128]{1,0:T(4,128)S(1)} %get-tuple-element.99, ...), kind=kOutput, calls=%fused_computation.10 | convolution fusion | flops 97055488 | bytes 11783168 | tf_op jit(solution)/shard_map/fxcy,cz->fxyz/dot_general | solution.py:41
  81.3 0.0 collective-permute-done.10
  81.3 0.0 collective-permute-done.11
  81.3 2.3 %collective-permute-start.12 = (f32[5,64,128]{2,1,0:T(8,128)S(1)}, f32[5,64,128]{2,1,0:T(8,128)S(1)}, u32[]{:S(2)}, u32[]{:S(2)}) collective-permute-start(f32[5,64,128]{2,1,0:T(8,128)S(1)} %multiply_add_fusion.4), channel_id=1, source_target_pairs={{0,128},{16,144},{32,160},{48,176},{64,192},{80,208},{96,224},{112... | collective-permute-start | bytes 491528 | tf_op jit(solution)/shard_map/ppermute | solution.py:99
  83.6 3.8 %collective-permute-start.13 = (f32[5,64,128]{2,1,0:T(8,128)S(1)}, f32[5,64,128]{2,1,0:T(8,128)S(1)}, u32[]{:S(2)}, u32[]{:S(2)}) collective-permute-start(f32[5,64,128]{2,1,0:T(8,128)S(1)} %multiply_add_fusion.3), channel_id=1, source_target_pairs={{0,128},{16,144},{32,160},{48,176},{64,192},{80,208},{96,224},{112... | collective-permute-start | bytes 491528 | tf_op jit(solution)/shard_map/ppermute | solution.py:99
  87.4 9.6 %collective-permute-done.12 = f32[5,64,128]{2,1,0:T(8,128)S(1)} collective-permute-done((f32[5,64,128]{2,1,0:T(8,128)S(1)}, f32[5,64,128]{2,1,0:T(8,128)S(1)}, u32[]{:S(2)}, u32[]{:S(2)}) %collective-permute-start.12) | collective-permute-done | bytes 163872 | tf_op jit(solution)/shard_map/ppermute | solution.py:99
  97.0 1.9 %collective-permute-done.13 = f32[5,64,128]{2,1,0:T(8,128)S(1)} collective-permute-done((f32[5,64,128]{2,1,0:T(8,128)S(1)}, f32[5,64,128]{2,1,0:T(8,128)S(1)}, u32[]{:S(2)}, u32[]{:S(2)}) %collective-permute-start.13) | collective-permute-done | bytes 163872 | tf_op jit(solution)/shard_map/ppermute | solution.py:99
  98.9 8.1 %fusion.16 = f32[5,32,64,128]{3,2,1,0:T(8,128)S(1)} fusion(f32[5,32,64,128]{3,2,1,0:T(8,128)} %multiply_subtract_fusion, f32[32,64,128]{2,1,0:T(8,128)S(1)} %multiply_bitcast_fusion, f32[5,64,128]{2,1,0:T(8,128)S(1)} %multiply_add_fusion.1, f32[32]{0:T(128)S(1)} %get-tuple-element.102, f32[5,64,128]{2,1,0:T(8,128)S(1)} %multiply_add_fusion.2, ...), kind=kOutput, calls=%fused_computation.18 | convolution fusion | flops 1013268480 | bytes 11868928 | tf_op jit(solution)/shard_map/fik,fxkz->fxiz/dot_general | solution.py:86
  107.0 0.1 slice.47
  107.1 3.4 %collective-permute-start.14 = (f32[5,32,128]{2,1,0:T(8,128)S(1)}, f32[5,32,128]{2,1,0:T(8,128)S(1)}, u32[]{:S(2)}, u32[]{:S(2)}) collective-permute-start(f32[5,32,128]{2,1,0:T(8,128)S(1)} %bitcast.55), channel_id=1, source_target_pairs={{0,4},{4,8},{8,12},{1,5},{5,9},{9,13},{2,6},{6,10},{10,14},{3,7},{... | collective-permute-start | bytes 245768 | tf_op jit(solution)/shard_map/ppermute | solution.py:59
  110.5 4.6 %collective-permute-start.15 = (f32[5,32,128]{2,1,0:T(8,128)S(1)}, f32[5,32,128]{2,1,0:T(8,128)S(1)}, u32[]{:S(2)}, u32[]{:S(2)}) collective-permute-start(f32[5,32,128]{2,1,0:T(8,128)S(1)} %bitcast.56), channel_id=1, source_target_pairs={{0,8},{4,12},{1,9},{5,13},{2,10},{6,14},{3,11},{7,15},{16,24},{20,... | collective-permute-start | bytes 245768 | tf_op jit(solution)/shard_map/ppermute | solution.py:59
  115.1 1.5 %collective-permute-start.16 = (f32[5,32,128]{2,1,0:T(8,128)S(1)}, f32[5,32,128]{2,1,0:T(8,128)S(1)}, u32[]{:S(2)}, u32[]{:S(2)}) collective-permute-start(f32[5,32,128]{2,1,0:T(8,128)S(1)} %bitcast.57), channel_id=1, source_target_pairs={{0,12},{1,13},{2,14},{3,15},{16,28},{17,29},{18,30},{19,31},{32,44... | collective-permute-start | bytes 245768 | tf_op jit(solution)/shard_map/ppermute | solution.py:59
  116.7 0.0 collective-permute-done.14
  116.7 0.5 collective-permute-done.15
  117.2 1.3 collective-permute-done.16
  118.5 0.1 multiply_add_fusion.10
  118.5 5.9 %fusion.19 = f32[5,32,64,128]{3,2,1,0:T(8,128)S(1)} fusion(f32[5,32,64,128]{3,2,1,0:T(8,128)S(1)} %fusion.16, f32[5,32,128]{2,1,0:T(8,128)S(1)} %multiply_add_fusion.10, f32[5,64]{1,0:T(8,128)S(1)} %get-tuple-element.88, f32[5,64]{1,0:T(8,128)S(1)} %get-tuple-element.76, f32[5,64]{1,0:T(8,128)S(1)} %fusion.53, pred[64,64]{1,0:T(8,128)(4,1)S(1)} %iota_compare_fusion), kind=kOutput, calls=%fused_computation.19 | convolution fusion | flops 1009315840 | bytes 10575616 | tf_op jit(solution)/shard_map/fik,fxkz->fxiz/dot_general | solution.py:91
  124.4 0.1 slice.48
  124.5 1.3 collective-permute-start.17
  125.8 1.3 collective-permute-start.18
  127.1 1.3 collective-permute-start.19
  128.4 2.4 %collective-permute-done.17 = f32[5,32,128]{2,1,0:T(8,128)S(1)} collective-permute-done((f32[5,32,128]{2,1,0:T(8,128)S(1)}, f32[5,32,128]{2,1,0:T(8,128)S(1)}, u32[]{:S(2)}, u32[]{:S(2)}) %collective-permute-start.17) | collective-permute-done | bytes 81952 | tf_op jit(solution)/shard_map/ppermute | solution.py:59
  130.9 2.9 %collective-permute-done.18 = f32[5,32,128]{2,1,0:T(8,128)S(1)} collective-permute-done((f32[5,32,128]{2,1,0:T(8,128)S(1)}, f32[5,32,128]{2,1,0:T(8,128)S(1)}, u32[]{:S(2)}, u32[]{:S(2)}) %collective-permute-start.18) | collective-permute-done | bytes 81952 | tf_op jit(solution)/shard_map/ppermute | solution.py:59
  133.8 3.0 %collective-permute-done.19 = f32[5,32,128]{2,1,0:T(8,128)S(1)} collective-permute-done((f32[5,32,128]{2,1,0:T(8,128)S(1)}, f32[5,32,128]{2,1,0:T(8,128)S(1)}, u32[]{:S(2)}, u32[]{:S(2)}) %collective-permute-start.19) | collective-permute-done | bytes 81952 | tf_op jit(solution)/shard_map/ppermute | solution.py:59
  136.7 0.1 multiply_add_fusion.9
  136.8 3.3 %multiply_add_fusion = f32[5,32,64,128]{3,2,1,0:T(8,128)} fusion(f32[5,32,64,128]{3,2,1,0:T(8,128)S(1)} %fusion.19, f32[5,32,128]{2,1,0:T(8,128)S(1)} %multiply_add_fusion.9, f32[5,64]{1,0:T(8,128)S(1)} %get-tuple-element.75), kind=kLoop, calls=%fused_computation | loop fusion | flops 2621440 | bytes 10568960 | tf_op jit(solution)/shard_map/add | solution.py:94
  (27 shorter events, 0.3 us)
Async XLA Ops:
  1.1 10.2 %collective-permute-start = (f32[5,2,64,128]{3,2,1,0:T(8,128)S(1)}, f32[5,2,64,128]{3,2,1,0:T(8,128)S(1)}, u32[]{:S(2)}, u32[]{:S(2)}) collective-permute-start(f32[5,2,64,128]{3,2,1,0:T(8,128)S(1)} %get-tuple-element.82), channel_id=1, source_target_pairs={{0,16},{16,32},{32,48},{48,64},{64,80},{80,96},{96,112},{112,128},... | collective-permute-start | bytes 983048 | tf_op jit(solution)/shard_map/ppermute | solution.py:99
  1.1 10.1 %collective-permute-start.1 = (f32[5,2,64,128]{3,2,1,0:T(8,128)S(1)}, f32[5,2,64,128]{3,2,1,0:T(8,128)S(1)}, u32[]{:S(2)}, u32[]{:S(2)}) collective-permute-start(f32[5,2,64,128]{3,2,1,0:T(8,128)S(1)} %get-tuple-element.81), channel_id=1, source_target_pairs={{0,240},{16,0},{32,16},{48,32},{64,48},{80,64},{96,80},{112,96},{1... | collective-permute-start | bytes 983048 | tf_op jit(solution)/shard_map/ppermute | solution.py:99
  11.3 0.7 copy-start.1
  12.0 0.7 copy-start.2
  34.3 36.8 %copy-start = (f32[5,32,64,128]{3,2,1,0:T(8,128)S(1)}, f32[5,32,64,128]{3,2,1,0:T(8,128)}, u32[]{:S(2)}) copy-start(f32[5,32,64,128]{3,2,1,0:T(8,128)} %get-tuple-element.62) | copy-start | bytes 15728644
  35.4 20.9 %collective-permute-start.4 = (f32[5,64,128]{2,1,0:T(8,128)S(1)}, f32[5,64,128]{2,1,0:T(8,128)S(1)}, u32[]{:S(2)}, u32[]{:S(2)}) collective-permute-start(f32[5,64,128]{2,1,0:T(8,128)S(1)} %slice_bitcast_fusion), channel_id=1, source_target_pairs={{0,16},{16,32},{32,48},{48,64},{64,80},{80,96},{96,112},{112,128},... | collective-permute-start | bytes 491528 | tf_op jit(solution)/shard_map/ppermute | solution.py:99
  35.4 20.9 %collective-permute-start.5 = (f32[5,64,128]{2,1,0:T(8,128)S(1)}, f32[5,64,128]{2,1,0:T(8,128)S(1)}, u32[]{:S(2)}, u32[]{:S(2)}) collective-permute-start(f32[5,64,128]{2,1,0:T(8,128)S(1)} %slice_bitcast_fusion), channel_id=1, source_target_pairs={{0,32},{16,48},{32,64},{48,80},{64,96},{80,112},{96,128},{112,144}... | collective-permute-start | bytes 491528 | tf_op jit(solution)/shard_map/ppermute | solution.py:99
  37.2 9.4 %collective-permute-start.2 = (f32[5,32,3,64]{3,2,1,0:T(4,128)S(1)}, f32[5,32,3,64]{3,2,1,0:T(4,128)S(1)}, u32[]{:S(2)}, u32[]{:S(2)}) collective-permute-start(f32[5,32,3,64]{3,2,1,0:T(4,128)S(1)} %get-tuple-element.84), channel_id=1, source_target_pairs={{0,1},{1,2},{2,3},{3,0},{4,5},{5,6},{6,7},{7,4},{8,9},{9,10},{10,1... | collective-permute-start | bytes 368648 | tf_op jit(solution)/shard_map/ppermute | solution.py:99
  38.5 17.8 %collective-permute-start.6 = (f32[5,64,128]{2,1,0:T(8,128)S(1)}, f32[5,64,128]{2,1,0:T(8,128)S(1)}, u32[]{:S(2)}, u32[]{:S(2)}) collective-permute-start(f32[5,64,128]{2,1,0:T(8,128)S(1)} %slice_bitcast_fusion.1), channel_id=1, source_target_pairs={{0,240},{16,0},{32,16},{48,32},{64,48},{80,64},{96,80},{112,96},{1... | collective-permute-start | bytes 491528 | tf_op jit(solution)/shard_map/ppermute | solution.py:99
  40.8 15.5 %collective-permute-start.7 = (f32[5,64,128]{2,1,0:T(8,128)S(1)}, f32[5,64,128]{2,1,0:T(8,128)S(1)}, u32[]{:S(2)}, u32[]{:S(2)}) collective-permute-start(f32[5,64,128]{2,1,0:T(8,128)S(1)} %slice_bitcast_fusion.1), channel_id=1, source_target_pairs={{0,224},{16,240},{32,0},{48,16},{64,32},{80,48},{96,64},{112,80},{... | collective-permute-start | bytes 491528 | tf_op jit(solution)/shard_map/ppermute | solution.py:99
  46.6 9.7 %collective-permute-start.3 = (f32[5,32,3,64]{3,2,1,0:T(4,128)S(1)}, f32[5,32,3,64]{3,2,1,0:T(4,128)S(1)}, u32[]{:S(2)}, u32[]{:S(2)}) collective-permute-start(f32[5,32,3,64]{3,2,1,0:T(4,128)S(1)} %get-tuple-element.83), channel_id=1, source_target_pairs={{0,3},{1,0},{2,1},{3,2},{4,7},{5,4},{6,5},{7,6},{8,11},{9,8},{10,9... | collective-permute-start | bytes 368648 | tf_op jit(solution)/shard_map/ppermute | solution.py:99
  56.4 7.0 %collective-permute-start.8 = (f32[5,64,128]{2,1,0:T(8,128)S(1)}, f32[5,64,128]{2,1,0:T(8,128)S(1)}, u32[]{:S(2)}, u32[]{:S(2)}) collective-permute-start(f32[5,64,128]{2,1,0:T(8,128)S(1)} %multiply_add_fusion.8), channel_id=1, source_target_pairs={{0,32},{16,48},{32,64},{48,80},{64,96},{80,112},{96,128},{112,144}... | collective-permute-start | bytes 491528 | tf_op jit(solution)/shard_map/ppermute | solution.py:99
  59.2 7.6 %collective-permute-start.9 = (f32[5,64,128]{2,1,0:T(8,128)S(1)}, f32[5,64,128]{2,1,0:T(8,128)S(1)}, u32[]{:S(2)}, u32[]{:S(2)}) collective-permute-start(f32[5,64,128]{2,1,0:T(8,128)S(1)} %multiply_add_fusion.7), channel_id=1, source_target_pairs={{0,224},{16,240},{32,0},{48,16},{64,32},{80,48},{96,64},{112,80},{... | collective-permute-start | bytes 491528 | tf_op jit(solution)/shard_map/ppermute | solution.py:99
  66.9 14.4 %collective-permute-start.10 = (f32[5,64,128]{2,1,0:T(8,128)S(1)}, f32[5,64,128]{2,1,0:T(8,128)S(1)}, u32[]{:S(2)}, u32[]{:S(2)}) collective-permute-start(f32[5,64,128]{2,1,0:T(8,128)S(1)} %multiply_add_fusion.6), channel_id=1, source_target_pairs={{0,64},{16,80},{32,96},{48,112},{64,128},{80,144},{96,160},{112,17... | collective-permute-start | bytes 491528 | tf_op jit(solution)/shard_map/ppermute | solution.py:99
  68.5 12.8 %collective-permute-start.11 = (f32[5,64,128]{2,1,0:T(8,128)S(1)}, f32[5,64,128]{2,1,0:T(8,128)S(1)}, u32[]{:S(2)}, u32[]{:S(2)}) collective-permute-start(f32[5,64,128]{2,1,0:T(8,128)S(1)} %multiply_add_fusion.5), channel_id=1, source_target_pairs={{0,192},{16,208},{32,224},{48,240},{64,0},{80,16},{96,32},{112,48}... | collective-permute-start | bytes 491528 | tf_op jit(solution)/shard_map/ppermute | solution.py:99
  81.3 15.6 %collective-permute-start.12 = (f32[5,64,128]{2,1,0:T(8,128)S(1)}, f32[5,64,128]{2,1,0:T(8,128)S(1)}, u32[]{:S(2)}, u32[]{:S(2)}) collective-permute-start(f32[5,64,128]{2,1,0:T(8,128)S(1)} %multiply_add_fusion.4), channel_id=1, source_target_pairs={{0,128},{16,144},{32,160},{48,176},{64,192},{80,208},{96,224},{112... | collective-permute-start | bytes 491528 | tf_op jit(solution)/shard_map/ppermute | solution.py:99
  83.6 15.2 %collective-permute-start.13 = (f32[5,64,128]{2,1,0:T(8,128)S(1)}, f32[5,64,128]{2,1,0:T(8,128)S(1)}, u32[]{:S(2)}, u32[]{:S(2)}) collective-permute-start(f32[5,64,128]{2,1,0:T(8,128)S(1)} %multiply_add_fusion.3), channel_id=1, source_target_pairs={{0,128},{16,144},{32,160},{48,176},{64,192},{80,208},{96,224},{112... | collective-permute-start | bytes 491528 | tf_op jit(solution)/shard_map/ppermute | solution.py:99
  107.1 9.6 %collective-permute-start.14 = (f32[5,32,128]{2,1,0:T(8,128)S(1)}, f32[5,32,128]{2,1,0:T(8,128)S(1)}, u32[]{:S(2)}, u32[]{:S(2)}) collective-permute-start(f32[5,32,128]{2,1,0:T(8,128)S(1)} %bitcast.55), channel_id=1, source_target_pairs={{0,4},{4,8},{8,12},{1,5},{5,9},{9,13},{2,6},{6,10},{10,14},{3,7},{... | collective-permute-start | bytes 245768 | tf_op jit(solution)/shard_map/ppermute | solution.py:59
  110.5 6.7 %collective-permute-start.15 = (f32[5,32,128]{2,1,0:T(8,128)S(1)}, f32[5,32,128]{2,1,0:T(8,128)S(1)}, u32[]{:S(2)}, u32[]{:S(2)}) collective-permute-start(f32[5,32,128]{2,1,0:T(8,128)S(1)} %bitcast.56), channel_id=1, source_target_pairs={{0,8},{4,12},{1,9},{5,13},{2,10},{6,14},{3,11},{7,15},{16,24},{20,... | collective-permute-start | bytes 245768 | tf_op jit(solution)/shard_map/ppermute | solution.py:59
  115.1 3.3 %collective-permute-start.16 = (f32[5,32,128]{2,1,0:T(8,128)S(1)}, f32[5,32,128]{2,1,0:T(8,128)S(1)}, u32[]{:S(2)}, u32[]{:S(2)}) collective-permute-start(f32[5,32,128]{2,1,0:T(8,128)S(1)} %bitcast.57), channel_id=1, source_target_pairs={{0,12},{1,13},{2,14},{3,15},{16,28},{17,29},{18,30},{19,31},{32,44... | collective-permute-start | bytes 245768 | tf_op jit(solution)/shard_map/ppermute | solution.py:59
  124.5 6.3 %collective-permute-start.17 = (f32[5,32,128]{2,1,0:T(8,128)S(1)}, f32[5,32,128]{2,1,0:T(8,128)S(1)}, u32[]{:S(2)}, u32[]{:S(2)}) collective-permute-start(f32[5,32,128]{2,1,0:T(8,128)S(1)} %bitcast.58), channel_id=1, source_target_pairs={{4,0},{8,4},{12,8},{5,1},{9,5},{13,9},{6,2},{10,6},{14,10},{7,3},{... | collective-permute-start | bytes 245768 | tf_op jit(solution)/shard_map/ppermute | solution.py:59
  125.8 7.9 %collective-permute-start.18 = (f32[5,32,128]{2,1,0:T(8,128)S(1)}, f32[5,32,128]{2,1,0:T(8,128)S(1)}, u32[]{:S(2)}, u32[]{:S(2)}) collective-permute-start(f32[5,32,128]{2,1,0:T(8,128)S(1)} %bitcast.59), channel_id=1, source_target_pairs={{8,0},{12,4},{9,1},{13,5},{10,2},{14,6},{11,3},{15,7},{24,16},{28,... | collective-permute-start | bytes 245768 | tf_op jit(solution)/shard_map/ppermute | solution.py:59
  127.1 9.6 %collective-permute-start.19 = (f32[5,32,128]{2,1,0:T(8,128)S(1)}, f32[5,32,128]{2,1,0:T(8,128)S(1)}, u32[]{:S(2)}, u32[]{:S(2)}) collective-permute-start(f32[5,32,128]{2,1,0:T(8,128)S(1)} %bitcast.60), channel_id=1, source_target_pairs={{12,0},{13,1},{14,2},{15,3},{28,16},{29,17},{30,18},{31,19},{44,32... | collective-permute-start | bytes 245768 | tf_op jit(solution)/shard_map/ppermute | solution.py:59
